TPU v7x, 1024 devices: a whole 4x4x32 slice. The times are simulated.
1024 devices in a mesh: dp: 128 (over z, x_hi, core), tp: 8 (over y, x_lo).
Axes of the slice: x: 4 (x_hi: 2, x_lo: 2; x = x_hi * 2 + x_lo), y: 4, z: 32, core: 2. Of those that a mesh axis runs over, the one named last changes fastest.
Arguments:
- hidden: bfloat16 [4, 6144, 8192], P(None, 'dp'), may hold values from -6 to 6
- kv_weight: bfloat16 [8192, 2048], P(('dp', 'tp')), may hold values from -0.0625 to 0.0625
- queries: bfloat16 [4, 6144, 8192], P(None, 'dp', 'tp'), may hold values from -6 to 6
- kv_cache: bfloat16 [6144, 8, 2, 96, 128], P('dp', 'tp'), may hold values from -6 to 6
- lengths: int32 [6144], P('dp'), may hold values from 2 to 92, as said below
- out_gain: bfloat16 [8192], replicated, may hold values from 0.5 to 1.5
Outputs:
- returned: bfloat16 [4, 6144, 8192], P(None, ('dp', 'tp'))
Inputs may be any that keep to these rules, and one draw needn't show every extreme that they name: `lengths`: some row has exactly 92 valid positions.
All inputs are finite; a program needn't handle non-finite values.
Results may differ from a plain program's by a relative error of at most 0.0085.
Values may be sent and summed in bfloat16 or wider, within the bound.
No kernel may reach another device: no remote copies, remote signals or barrier semaphores. Data moves between devices by JAX's collectives and lax.ppermute only.
A program may use at most 32 MiB of HBM per device.

v0:
```python
import jax
import jax.numpy as jnp
from jax import lax
from jax.sharding import Mesh
from jax.sharding import PartitionSpec as P

DP = ("dp_0", "dp_1", "dp_2")
DP_TP = ("dp_0", "dp_1", "dp_2", "tp")


def in_order(tiles, dim):
    shape = list(tiles.shape[1:])
    shape[dim] *= tiles.shape[0]
    return jnp.moveaxis(tiles, 0, dim).reshape(shape)


def all_blocks(value, axes, sequence):
    tiles = value
    for k in sequence:
        tiles = lax.all_gather(tiles, axes[k])
    done = sequence[::-1]
    back = [done.index(k) for k in range(len(axes))]
    tiles = tiles.transpose(*back, *range(len(axes), tiles.ndim))
    return tiles.reshape(-1, *value.shape)


def gathered_by_axis(value, axes, sequence, dim):
    return in_order(all_blocks(value, axes, sequence), dim)


def per_device(hidden, kv_weight, queries, kv_cache, lengths, out_gain):
    steps, rows, width = hidden.shape
    local_groups = kv_cache.shape[1]
    own_piece = lax.all_to_all(kv_weight, "tp", split_axis=1, concat_axis=0, tiled=True)
    flat_rows = hidden.reshape(steps * rows, width)
    projected = jnp.dot(
        flat_rows, gathered_by_axis(own_piece, DP, (1, 0, 2), 0), preferred_element_type=jnp.float32
    )
    head_size = kv_cache.shape[4]
    fresh = projected.astype(jnp.bfloat16).reshape(steps, rows, local_groups, 2, head_size)
    per_group = queries.shape[2] // (local_groups * head_size)
    query = queries.reshape(steps, rows, local_groups, per_group, head_size)
    scale = 1.0 / jnp.sqrt(jnp.float32(head_size))
    cache_len = kv_cache.shape[3]
    valid = jnp.arange(cache_len)[None, :] < lengths[:, None]
    causal = jnp.arange(steps)[:, None] >= jnp.arange(steps)[None, :]
    old_scores = (
        jnp.einsum(
            "srgpe,rgce->srgpc", query, kv_cache[:, :, 0], preferred_element_type=jnp.float32
        )
        * scale
    )
    old_scores = jnp.where(valid[None, :, None, None, :], old_scores, -1e30)
    new_scores = (
        jnp.einsum(
            "srgpe,trge->srgpt", query, fresh[:, :, :, 0], preferred_element_type=jnp.float32
        )
        * scale
    )
    new_scores = jnp.where(causal[:, None, None, None, :], new_scores, -1e30)
    top = jnp.maximum(
        jnp.max(old_scores, -1, keepdims=True), jnp.max(new_scores, -1, keepdims=True)
    )
    old_exp = jnp.exp(old_scores - top)
    new_exp = jnp.exp(new_scores - top)
    total = jnp.sum(old_exp, -1, keepdims=True) + jnp.sum(new_exp, -1, keepdims=True)
    old_weights = (old_exp / total).astype(jnp.bfloat16)
    new_weights = (new_exp / total).astype(jnp.bfloat16)
    mixed = jnp.einsum(
        "srgpc,rgce->srgpe", old_weights, kv_cache[:, :, 1], preferred_element_type=jnp.float32
    )
    mixed = mixed + jnp.einsum(
        "srgpt,trge->srgpe", new_weights, fresh[:, :, :, 1], preferred_element_type=jnp.float32
    )
    attn = mixed.astype(jnp.bfloat16).reshape(steps, rows, local_groups * per_group * head_size)
    arrived = lax.all_to_all(attn, "tp", split_axis=1, concat_axis=2, tiled=True)
    values = arrived.astype(jnp.float32)
    square_mean = jnp.mean(values * values, -1, keepdims=True)
    normed = values * lax.rsqrt(square_mean + 1e-05) * out_gain.astype(jnp.float32)
    return normed.astype(jnp.bfloat16)


def solution(mesh):
    torus = Mesh(mesh.devices.reshape(32, 2, 2, mesh.shape["tp"]), ("dp_0", "dp_1", "dp_2", "tp"))
    return jax.shard_map(
        per_device,
        mesh=torus,
        in_specs=(
            P(None, DP, None),
            P(DP_TP, None),
            P(None, DP, "tp"),
            P(DP, "tp", None, None, None),
            P(DP),
            P(),
        ),
        out_specs=P(None, DP_TP, None),
        check_vma=False,
    )
```

profile of v0, /device:TPU:1, one launch (start us, length us, event | category | flops | bytes accessed | tf_op | source)
XLA Modules:
  0.0 236.7 jit_solution(15302083519382822985)
XLA Ops:
  6.5 0.0 copy-start
  6.5 0.0 copy-start.2
  6.5 0.0 copy-start.5
  6.5 0.0 all-gather.5.cloned.1.call-start
  6.5 11.3 %all_to_all.25 = bf16[8,8,256]{2,0,1:T(8,128)(2,1)S(1)} all-to-all(bf16[8,8,256]{2,0,1:T(8,128)(2,1)} %bitcast.119), channel_id=1, replica_groups=mesh['dp_0'=32,'dp_1'=2,'dp_2'=2,'tp'=8] {'tp'}, dimensions={1} | all-to-all | bytes 65536 | tf_op jit(solution)/shard_map/all_to_all | solution.py:34
  17.9 5.0 %all_gather.19 = bf16[2,64,256]{2,1,0:T(8,128)(2,1)} all-gather(bf16[1,64,256]{2,1,0:T(8,128)(2,1)S(1)} %bitcast.118), channel_id=1, replica_groups=mesh['dp_0'=32,'dp_1'=2,'dp_2'=2,'tp'=8] {'dp_1'}, dimensions={0}, use_global_device_ids=true | all-gather | bytes 98304 | tf_op jit(solution)/shard_map/all_gather | solution.py:20
  22.9 0.0 all-gather.5.cloned.1.call-update
  22.9 0.0 all-gather.7.cloned.1.call-start
  23.0 125.6 %all-gather.5.cloned.1.call-done = bf16[64,64,256]{2,1,0:T(8,128)(2,1)} async-done(((bf16[2,64,256]{2,1,0:T(8,128)(2,1)}), bf16[64,64,256]{2,1,0:T(8,128)(2,1)}) %all-gather.5.cloned.1.call-update) | async-done | bytes 2097168 | tf_op jit(solution)/shard_map/all_gather | solution.py:20
  148.6 0.0 all-gather.7.cloned.1.call-update
  148.6 0.0 copy-done.2
  148.6 0.1 copy.47
  148.7 0.0 copy-start.3
  148.7 0.0 copy-done.5
  148.7 0.1 iota_compare_fusion
  148.8 0.6 copy-done.3
  149.4 2.9 %fusion.22 = (f32[4,48,8]{2,0,1:T(4,128)S(1)}, f32[4,48,1,8,96]{4,3,0,1,2:T(8,128)}) fusion(bf16[48,1,2,96,128]{4,3,2,1,0:T(8,128)(2,1)} %param.9, pred[48,96]{1,0:T(8,128)(4,1)S(1)} %iota_compare_fusion, bf16[4,48,8,128]{3,2,1,0:T(8,128)(2,1)S(1)} %bitcast.116), kind=kOutput, calls=%fused_computation.38 | convolution fusion | flops 38189568 | bytes 2173440 | tf_op jit(solution)/shard_map/srgpe,rgce->srgpc/dot_general | solution.py:48
  152.4 47.8 %all-gather.7.cloned.1.call-done = bf16[64,2,64,256]{3,2,1,0:T(8,128)(2,1)} async-done(((bf16[32,2,64,256]{3,2,1,0:T(8,128)(2,1)}), bf16[64,2,64,256]{3,2,1,0:T(8,128)(2,1)}) %all-gather.7.cloned.1.call-update) | async-done | bytes 4194320 | tf_op jit(solution)/shard_map/all_gather | solution.py:20
  200.2 2.5 %copy.31 = bf16[32,2,2,64,256]{4,3,2,1,0:T(8,128)(2,1)S(1)} copy(bf16[32,2,2,64,256]{4,3,1,0,2:T(8,128)(2,1)} %bitcast.111) | data formatting | bytes 8388608 | tf_op jit(solution)/shard_map/transpose | solution.py:23
  202.7 0.0 copy-done
  202.7 1.1 convolution_convert_fusion
  203.8 0.0 copy-start.1
  203.9 0.1 fusion.21
  204.0 2.9 %fusion.23 = (f32[4,48,8]{2,0,1:T(4,128)S(1)}, f32[4,48,1,8,4]{3,4,0,1,2:T(4,128)S(1)}) fusion(bf16[4,48,1,1,128]{4,3,1,0,2:T(2,128)(2,1)S(1)} %get-tuple-element.6, pred[4,4]{1,0:T(4,128)(4,1)S(1)} %iota_compare_fusion.1, bf16[4,48,8,128]{3,2,1,0:T(8,128)(2,1)} %bitcast.117), kind=kOutput, calls=%fused_computation.39 | convolution fusion | flops 1589760 | bytes 473104 | tf_op jit(solution)/shard_map/srgpe,trge->srgpt/dot_general | solution.py:55
  207.0 0.4 fusion.17
  207.4 0.0 copy-start.6
  207.4 0.0 copy-done.1
  207.4 0.6 fusion.12
  208.0 0.4 fusion.18
  208.4 0.6 copy-done.6
  209.0 0.0 copy-start.4
  209.0 0.6 fusion.5
  209.6 0.8 reshape.144
  210.5 3.5 %all-to-all-start.1 = ((bf16[4,48,1024]{2,0,1:T(4,128)(2,1)}), bf16[4,48,1024]{2,0,1:T(4,128)(2,1)S(1)}, u32[]{:S(2)}, u32[]{:S(2)}) async-start(bf16[4,48,1024]{2,0,1:T(4,128)(2,1)} %reshape.144), calls=%async_computation.1 | async-start | bytes 786432 | tf_op jit(solution)/shard_map/all_to_all | solution.py:76
  213.9 0.0 copy-done.4
  213.9 0.6 convert_element_type.52
  214.5 7.6 %all-to-all-done.1 = bf16[4,48,1024]{2,0,1:T(4,128)(2,1)S(1)} async-done(((bf16[4,48,1024]{2,0,1:T(4,128)(2,1)}), bf16[4,48,1024]{2,0,1:T(4,128)(2,1)S(1)}, u32[]{:S(2)}, u32[]{:S(2)}) %all-to-all-start.1) | async-done | bytes 393248 | tf_op jit(solution)/shard_map/all_to_all | solution.py:76
  222.1 1.1 copy.63
  223.3 2.5 %reshape.145 = f32[4,6,8192]{2,0,1:T(4,128)} reshape(f32[4,6,8,1024]{3,2,0,1:T(8,128)} %bitcast.113) | data formatting | bytes 1572864 | tf_op jit(solution)/shard_map/convert_element_type | solution.py:77
  225.8 0.9 multiply_reduce_fusion
  226.7 0.8 copy.37
  227.5 0.1 reduce_sum.37
  227.6 0.1 copy.38
  227.7 2.1 multiply_convert_fusion
  (6 shorter events, 0.1 us)
Async XLA Ops:
  6.5 196.2 %copy-start = (bf16[4,48,8192]{2,1,0:T(8,128)(2,1)S(1)}, bf16[4,48,8192]{2,1,0:T(8,128)(2,1)}, u32[]{:S(2)}) copy-start(bf16[4,48,8192]{2,1,0:T(8,128)(2,1)} %param.6) | copy-start | bytes 9437188
  6.5 142.1 %copy-start.2 = (bf16[4,48,1024]{2,1,0:T(8,128)(2,1)S(1)}, bf16[4,48,1024]{2,1,0:T(8,128)(2,1)}, u32[]{:S(2)}) copy-start(bf16[4,48,1024]{2,1,0:T(8,128)(2,1)} %param.8) | copy-start | bytes 1179652
  6.5 142.2 %copy-start.5 = (s32[48]{0:T(128)S(1)}, s32[48]{0:T(128)}, u32[]{:S(2)}) copy-start(s32[48]{0:T(128)} %param.10) | copy-start | bytes 580
  6.5 142.0 %all-gather.5.cloned.1.call-start = ((), (), s32[]{:S(2)}) async-start(), calls=%async_computation.2 | async-start | bytes 2162688 | tf_op jit(solution)/shard_map/all_gather | solution.py:20
  22.9 177.3 %all-gather.7.cloned.1.call-start = ((), (), s32[]{:S(2)}) async-start(), calls=%async_computation.3 | async-start | bytes 6291456 | tf_op jit(solution)/shard_map/all_gather | solution.py:20
  148.7 0.7 copy-start.3
  203.8 3.5 %copy-start.1 = (f32[4,48,1,8,96]{4,3,0,1,2:T(8,128)S(1)}, f32[4,48,1,8,96]{4,3,0,1,2:T(8,128)}, u32[]{:S(2)}) copy-start(f32[4,48,1,8,96]{4,3,0,1,2:T(8,128)} %get-tuple-element.8) | copy-start | bytes 1769476
  207.4 1.7 copy-start.6
  209.0 4.9 %copy-start.4 = (bf16[8192]{0:T(1024)(128)(2,1)S(1)}, bf16[8192]{0:T(1024)(128)(2,1)}, u32[]{:S(2)}) copy-start(bf16[8192]{0:T(1024)(128)(2,1)} %param.11) | copy-start | bytes 49156
  210.5 11.7 %all-to-all-start.1 = ((bf16[4,48,1024]{2,0,1:T(4,128)(2,1)}), bf16[4,48,1024]{2,0,1:T(4,128)(2,1)S(1)}, u32[]{:S(2)}, u32[]{:S(2)}) async-start(bf16[4,48,1024]{2,0,1:T(4,128)(2,1)} %reshape.144), calls=%async_computation.1 | async-start | bytes 786432 | tf_op jit(solution)/shard_map/all_to_all | solution.py:76
Sparse Core Ops, SparseCore 0:
  23.0 125.4 all-gather.4
  151.2 48.9 all-gather.6
where the time goes:
time: 237 us
  waiting for transfers between devices  181 us (76%)
  blocking collectives  16.3 us (7%)
  between operations  13.6 us (6%)
  local copies, waits for them, and re-layouts  9.5 us (4%)
  matrix products  7.97 us (3%)
  other arithmetic  4.76 us (2%)
  starting transfers between devices  3.5 us (1%)
    all_gather x2, waiting for transfers between devices, all_blocks(): tiles = lax.all_gather(tiles, axes[k])  173 us
    all_to_all x1, blocking collectives, per_device(): lax.all_to_all(kv_weight, 'tp', split_axis=1, concat_axis=0, tiled=True)  11.3 us
    all_to_all x1, waiting for transfers between devices, per_device(): lax.all_to_all(attn, 'tp', split_axis=1, concat_axis=2, tiled=True)  7.58 us
    all_gather x1, blocking collectives, all_blocks(): tiles = lax.all_gather(tiles, axes[k])  5.03 us
  transfers between devices with their start and end apart: 3, of which 3 were waited for; matrix products, arithmetic and copies ran while one was open for 2% of the time, Pallas kernels for 0%

commit v1 on v0

--- a/solution.py
+++ b/solution.py
@@ -34,7 +34,7 @@
     own_piece = lax.all_to_all(kv_weight, "tp", split_axis=1, concat_axis=0, tiled=True)
     flat_rows = hidden.reshape(steps * rows, width)
     projected = jnp.dot(
-        flat_rows, gathered_by_axis(own_piece, DP, (1, 0, 2), 0), preferred_element_type=jnp.float32
+        flat_rows, gathered_by_axis(own_piece, DP, (2, 1, 0), 0), preferred_element_type=jnp.float32
     )
     head_size = kv_cache.shape[4]
     fresh = projected.astype(jnp.bfloat16).reshape(steps, rows, local_groups, 2, head_size)

time: 237 us -> 213 us (0.90)
  the two profiles are of different devices: /device:TPU:1 before, /device:TPU:4 now
where the time goes in v1:
time: 213 us; the launch traced here: 212 us
  waiting for transfers between devices  143 us (67%)
  blocking collectives  27.9 us (13%)
  between operations  13.5 us (6%)
  matrix products  10 us (5%)
  local copies, waits for them, and re-layouts  7.36 us (3%)
  other arithmetic  5.45 us (3%)
  starting transfers between devices  5.23 us (2%)
    all_gather x1, waiting for transfers between devices, all_blocks(): tiles = lax.all_gather(tiles, axes[k])  135 us
    all_gather x2, blocking collectives, all_blocks(): tiles = lax.all_gather(tiles, axes[k])  16.3 us
    all_to_all x1, blocking collectives, per_device(): lax.all_to_all(kv_weight, 'tp', split_axis=1, concat_axis=0, tiled=True)  11.6 us
    all_to_all x1, waiting for transfers between devices, per_device(): lax.all_to_all(attn, 'tp', split_axis=1, concat_axis=2, tiled=True)  7.38 us
    all_to_all x1, starting transfers between devices, per_device(): lax.all_to_all(attn, 'tp', split_axis=1, concat_axis=2, tiled=True)  5.23 us
  transfers between devices with their start and end apart: 2, of which 2 were waited for; matrix products, arithmetic and copies ran while one was open for 3% of the time, Pallas kernels for 0%

profile of v1, /device:TPU:4, one launch (start us, length us, event | category | flops | bytes accessed | tf_op | source)
XLA Modules:
  0.0 212.4 jit_solution(17328605873707488403)
XLA Ops:
  6.5 0.0 copy-start
  6.5 0.0 all-gather.4.cloned.1.call-start
  6.5 11.6 %all_to_all.25 = bf16[8,8,256]{2,0,1:T(8,128)(2,1)S(1)} all-to-all(bf16[8,8,256]{2,0,1:T(8,128)(2,1)} %bitcast.115), channel_id=1, replica_groups=mesh['dp_0'=32,'dp_1'=2,'dp_2'=2,'tp'=8] {'tp'}, dimensions={1} | all-to-all | bytes 65536 | tf_op jit(solution)/shard_map/all_to_all | solution.py:34
  18.2 1.8 all_gather.19
  20.0 14.4 %all-gather = bf16[4,64,256]{2,1,0:T(8,128)(2,1)} all-gather(bf16[2,64,256]{2,1,0:T(8,128)(2,1)S(1)} %all_gather.19), channel_id=2, replica_groups=mesh['dp_0'=32,'dp_1'=2,'dp_2'=2,'tp'=8] {'dp_1'}, dimensions={0}, use_global_device_ids=true | all-gather | bytes 196608 | tf_op jit(solution)/shard_map/all_gather | solution.py:20
  34.4 0.0 all-gather.4.cloned.1.call-update
  34.5 1.1 copy.38
  35.5 0.0 copy-start.2
  35.5 0.8 iota_compare_fusion
  36.3 0.0 copy-done.2
  36.3 2.9 %fusion.22 = (f32[4,48,8]{2,0,1:T(4,128)S(1)}, f32[4,48,1,8,96]{4,3,0,1,2:T(8,128)}) fusion(bf16[48,1,2,96,128]{4,3,2,1,0:T(8,128)(2,1)} %param.9, pred[48,96]{1,0:T(8,128)(4,1)S(1)} %iota_compare_fusion, bf16[4,48,8,128]{3,2,1,0:T(8,128)(2,1)S(1)} %bitcast.112), kind=kOutput, calls=%fused_computation.38 | convolution fusion | flops 38189568 | bytes 2173440 | tf_op jit(solution)/shard_map/srgpe,rgce->srgpc/dot_general | solution.py:48
  39.3 135.5 %all-gather.4.cloned.1.call-done = bf16[64,2,64,256]{3,2,1,0:T(8,128)(2,1)} async-done(((bf16[2,2,64,256]{3,2,1,0:T(8,128)(2,1)}), bf16[64,2,64,256]{3,2,1,0:T(8,128)(2,1)}) %all-gather.4.cloned.1.call-update) | async-done | bytes 4194320 | tf_op jit(solution)/shard_map/all_gather | solution.py:20
  174.8 0.0 copy-done
  174.8 3.2 %convolution_convert_fusion = bf16[192,256]{1,0:T(8,128)(2,1)S(1)} fusion(bf16[192,8192]{1,0:T(8,128)(2,1)S(1)} %bitcast.106, bf16[8192,256]{1,0:T(8,128)(2,1)} %bitcast.107), kind=kOutput, calls=%fused_computation.14 | convolution fusion | flops 805355520 | bytes 7438336 | tf_op jit(solution)/shard_map/dot_general | solution.py:36
  178.0 0.0 copy-start.1
  178.0 0.1 fusion.21
  178.1 2.9 %fusion.23 = (f32[4,48,8]{2,0,1:T(4,128)S(1)}, f32[4,48,1,8,4]{3,4,0,1,2:T(4,128)S(1)}) fusion(bf16[4,48,1,1,128]{4,3,1,0,2:T(2,128)(2,1)S(1)} %get-tuple-element.6, pred[4,4]{1,0:T(4,128)(4,1)S(1)} %iota_compare_fusion.1, bf16[4,48,8,128]{3,2,1,0:T(8,128)(2,1)} %bitcast.113), kind=kOutput, calls=%fused_computation.39 | convolution fusion | flops 1589760 | bytes 473104 | tf_op jit(solution)/shard_map/srgpe,trge->srgpt/dot_general | solution.py:55
  181.1 0.4 fusion.17
  181.5 0.0 copy-start.4
  181.5 0.0 copy-done.1
  181.5 0.6 fusion.12
  182.1 0.4 fusion.18
  182.5 0.6 copy-done.4
  183.1 0.0 copy-start.3
  183.1 0.6 fusion.5
  183.7 0.8 reshape.144
  184.6 5.2 %all-to-all-start.1 = ((bf16[4,48,1024]{2,0,1:T(4,128)(2,1)}), bf16[4,48,1024]{2,0,1:T(4,128)(2,1)S(1)}, u32[]{:S(2)}, u32[]{:S(2)}) async-start(bf16[4,48,1024]{2,0,1:T(4,128)(2,1)} %reshape.144), calls=%async_computation.1 | async-start | bytes 786432 | tf_op jit(solution)/shard_map/all_to_all | solution.py:76
  189.8 0.0 copy-done.3
  189.8 0.6 convert_element_type.52
  190.4 7.4 %all-to-all-done.1 = bf16[4,48,1024]{2,0,1:T(4,128)(2,1)S(1)} async-done(((bf16[4,48,1024]{2,0,1:T(4,128)(2,1)}), bf16[4,48,1024]{2,0,1:T(4,128)(2,1)S(1)}, u32[]{:S(2)}, u32[]{:S(2)}) %all-to-all-start.1) | async-done | bytes 393248 | tf_op jit(solution)/shard_map/all_to_all | solution.py:76
  197.8 1.1 copy.54
  198.9 2.5 %reshape.145 = f32[4,6,8192]{2,0,1:T(4,128)} reshape(f32[4,6,8,1024]{3,2,0,1:T(8,128)} %bitcast.109) | data formatting | bytes 1572864 | tf_op jit(solution)/shard_map/convert_element_type | solution.py:77
  201.5 0.9 multiply_reduce_fusion
  202.4 0.8 copy.28
  203.2 0.1 reduce_sum.37
  203.3 0.1 copy.29
  203.4 2.1 %multiply_convert_fusion = bf16[4,6,8192]{2,0,1:T(4,128)(2,1)} fusion(f32[4,6,8192]{2,0,1:T(4,128)} %reshape.145, f32[8192]{0:T(1024)} %convert_element_type.52, f32[4,6]{0,1:T(8,128)S(1)} %copy.29), kind=kLoop, calls=%fused_computation.17 | loop fusion | flops 589824 | bytes 1212512 | tf_op jit(solution)/shard_map/convert_element_type | solution.py:80
  (6 shorter events, 0.1 us)
Async XLA Ops:
  6.5 168.2 %copy-start = (bf16[4,48,8192]{2,1,0:T(8,128)(2,1)S(1)}, bf16[4,48,8192]{2,1,0:T(8,128)(2,1)}, u32[]{:S(2)}) copy-start(bf16[4,48,8192]{2,1,0:T(8,128)(2,1)} %param.6) | copy-start | bytes 9437188
  6.5 168.2 %all-gather.4.cloned.1.call-start = ((), (), s32[]{:S(2)}) async-start(), calls=%async_computation.2 | async-start | bytes 4325376 | tf_op jit(solution)/shard_map/all_gather | solution.py:20
  35.5 0.8 copy-start.2
  178.0 3.5 %copy-start.1 = (f32[4,48,1,8,96]{4,3,0,1,2:T(8,128)S(1)}, f32[4,48,1,8,96]{4,3,0,1,2:T(8,128)}, u32[]{:S(2)}) copy-start(f32[4,48,1,8,96]{4,3,0,1,2:T(8,128)} %get-tuple-element.8) | copy-start | bytes 1769476
  181.5 1.7 copy-start.4
  183.1 6.7 %copy-start.3 = (bf16[8192]{0:T(1024)(128)(2,1)S(1)}, bf16[8192]{0:T(1024)(128)(2,1)}, u32[]{:S(2)}) copy-start(bf16[8192]{0:T(1024)(128)(2,1)} %param.11) | copy-start | bytes 49156
  184.6 13.2 %all-to-all-start.1 = ((bf16[4,48,1024]{2,0,1:T(4,128)(2,1)}), bf16[4,48,1024]{2,0,1:T(4,128)(2,1)S(1)}, u32[]{:S(2)}, u32[]{:S(2)}) async-start(bf16[4,48,1024]{2,0,1:T(4,128)(2,1)} %reshape.144), calls=%async_computation.1 | async-start | bytes 786432 | tf_op jit(solution)/shard_map/all_to_all | solution.py:76
Sparse Core Ops, SparseCore 0:
  34.6 140.1 all-gather.3

commit v2 on v1

--- a/solution.py
+++ b/solution.py
@@ -4,8 +4,8 @@
 from jax.sharding import Mesh
 from jax.sharding import PartitionSpec as P
 
-DP = ("dp_0", "dp_1", "dp_2")
-DP_TP = ("dp_0", "dp_1", "dp_2", "tp")
+DP = ("dp_0a", "dp_0b", "dp_1", "dp_2")
+DP_TP = ("dp_0a", "dp_0b", "dp_1", "dp_2", "tp")
 
 
 def in_order(tiles, dim):
@@ -28,13 +28,28 @@
     return in_order(all_blocks(value, axes, sequence), dim)
 
 
+def pp_gather(x, axis, n):
+    me = lax.axis_index(axis)
+    pieces = [x] + [lax.ppermute(x, axis, [(k, (k + d) % n) for k in range(n)]) for d in range(1, n)]
+    rel = jnp.stack(pieces)
+    return jnp.take(rel, (me - jnp.arange(n)) % n, axis=0)
+
+
+def gather_w(own_piece, zb_pp, core_pp):
+    t = lax.all_gather(own_piece, "dp_1")
+    t = lax.all_gather(t, "dp_0a")
+    t = pp_gather(t, "dp_0b", 4) if zb_pp else lax.all_gather(t, "dp_0b")
+    t = pp_gather(t, "dp_2", 2) if core_pp else lax.all_gather(t, "dp_2")
+    return t.transpose(2, 1, 3, 0, 4, 5).reshape(-1, own_piece.shape[1])
+
+
 def per_device(hidden, kv_weight, queries, kv_cache, lengths, out_gain):
     steps, rows, width = hidden.shape
     local_groups = kv_cache.shape[1]
     own_piece = lax.all_to_all(kv_weight, "tp", split_axis=1, concat_axis=0, tiled=True)
     flat_rows = hidden.reshape(steps * rows, width)
     projected = jnp.dot(
-        flat_rows, gathered_by_axis(own_piece, DP, (2, 1, 0), 0), preferred_element_type=jnp.float32
+        flat_rows, gather_w(own_piece, True, True), preferred_element_type=jnp.float32
     )
     head_size = kv_cache.shape[4]
     fresh = projected.astype(jnp.bfloat16).reshape(steps, rows, local_groups, 2, head_size)
@@ -81,7 +96,7 @@
 
 
 def solution(mesh):
-    torus = Mesh(mesh.devices.reshape(32, 2, 2, mesh.shape["tp"]), ("dp_0", "dp_1", "dp_2", "tp"))
+    torus = Mesh(mesh.devices.reshape(8, 4, 2, 2, mesh.shape["tp"]), ("dp_0a", "dp_0b", "dp_1", "dp_2", "tp"))
     return jax.shard_map(
         per_device,
         mesh=torus,

time: 213 us -> 181 us (0.85)
  the two profiles are of different devices: /device:TPU:4 before, /device:TPU:32 now
where the time goes in v2:
time: 181 us; the launch traced here: 180 us
  blocking collectives  75.4 us (42%)
  waiting for transfers between devices  43.7 us (24%)
  other arithmetic  18.7 us (10%)
  local copies, waits for them, and re-layouts  18.6 us (10%)
  starting transfers between devices  15.6 us (9%)
  matrix products  7.97 us (4%)
    all_gather x1, blocking collectives, gather_w(): t = lax.all_gather(t, 'dp_0a')  57.4 us
    ppermute x4, waiting for transfers between devices, pp_gather(): lax.ppermute(x, axis, [(k, (k + d) % n) for k in range(n)])  35.2 us
    ppermute x4, starting transfers between devices, pp_gather(): lax.ppermute(x, axis, [(k, (k + d) % n) for k in range(n)])  12.1 us
    all_to_all x1, blocking collectives, per_device(): lax.all_to_all(kv_weight, 'tp', split_axis=1, concat_axis=0, tiled=True)  11.9 us
    gather x3, local copies, waits for them, and re-layouts, pp_gather(): return jnp.take(rel, (me - jnp.arange(n)) % n, axis=0)  11.1 us
    all_to_all x1, waiting for transfers between devices, per_device(): lax.all_to_all(attn, 'tp', split_axis=1, concat_axis=2, tiled=True)  8.57 us
    another operation x2, other arithmetic, pp_gather(): rel = jnp.stack(pieces)  7.16 us
    select_n x5, other arithmetic, pp_gather(): return jnp.take(rel, (me - jnp.arange(n)) % n, axis=0)  6.71 us
  transfers between devices with their start and end apart: 5, of which 5 were waited for; matrix products, arithmetic and copies ran while one was open for 2% of the time, Pallas kernels for 0%

profile of v2, /device:TPU:32, one launch (start us, length us, event | category | flops | bytes accessed | tf_op | source)
XLA Modules:
  0.0 180.2 jit_solution(7514574067849434107)
XLA Ops:
  0.0 0.0 copy-start
  0.0 11.9 %all_to_all.25 = bf16[8,8,256]{2,0,1:T(8,128)(2,1)S(1)} all-to-all(bf16[8,8,256]{2,0,1:T(8,128)(2,1)} %bitcast.129), channel_id=1, replica_groups=mesh['dp_0a'=8,'dp_0b'=4,'dp_1'=2,'dp_2'=2,'tp'=8] {'tp'}, dimensions={1} | all-to-all | bytes 65536 | tf_op jit(solution)/shard_map/all_to_all | solution.py:49
  11.9 6.1 %all_gather.13 = bf16[2,64,256]{2,1,0:T(8,128)(2,1)S(1)} all-gather(bf16[1,64,256]{2,1,0:T(8,128)(2,1)S(1)} %bitcast.128), channel_id=1, replica_groups=mesh['dp_0a'=8,'dp_0b'=4,'dp_1'=2,'dp_2'=2,'tp'=8] {'dp_1'}, dimensions={0}, use_global_device_ids=true | all-gather | bytes 98304 | tf_op jit(solution)/shard_map/all_gather | solution.py:39
  18.0 57.4 %all-gather = bf16[16,64,256]{2,1,0:T(8,128)(2,1)} all-gather(bf16[2,64,256]{2,1,0:T(8,128)(2,1)S(1)} %all_gather.13), channel_id=2, replica_groups=mesh['dp_0a'=8,'dp_0b'=4,'dp_1'=2,'dp_2'=2,'tp'=8] {'dp_0a'}, dimensions={0}, use_global_device_ids=true | all-gather | bytes 589824 | tf_op jit(solution)/shard_map/all_gather | solution.py:40
  75.4 2.1 %collective-permute-start = (bf16[8,2,64,256]{3,2,1,0:T(8,128)(2,1)}, bf16[8,2,64,256]{3,2,1,0:T(8,128)(2,1)}, u32[]{:S(2)}, u32[]{:S(2)}) collective-permute-start(bf16[8,2,64,256]{3,2,1,0:T(8,128)(2,1)} %bitcast.9), channel_id=1, source_target_pairs={{0,32},{32,64},{64,96},{96,0},{1,33},{33,65},{65,97},{97,1},{2,34}... | collective-permute-start | bytes 1572872 | tf_op jit(solution)/shard_map/ppermute | solution.py:33
  77.5 6.1 %collective-permute-start.1 = (bf16[8,2,64,256]{3,2,1,0:T(8,128)(2,1)}, bf16[8,2,64,256]{3,2,1,0:T(8,128)(2,1)}, u32[]{:S(2)}, u32[]{:S(2)}) collective-permute-start(bf16[8,2,64,256]{3,2,1,0:T(8,128)(2,1)} %bitcast.9), channel_id=1, source_target_pairs={{0,64},{32,96},{64,0},{96,32},{1,65},{33,97},{65,1},{97,33},{2,66}... | collective-permute-start | bytes 1572872 | tf_op jit(solution)/shard_map/ppermute | solution.py:33
  83.7 1.9 %collective-permute-start.2 = (bf16[8,2,64,256]{3,2,1,0:T(8,128)(2,1)}, bf16[8,2,64,256]{3,2,1,0:T(8,128)(2,1)}, u32[]{:S(2)}, u32[]{:S(2)}) collective-permute-start(bf16[8,2,64,256]{3,2,1,0:T(8,128)(2,1)} %bitcast.9), channel_id=1, source_target_pairs={{0,96},{32,0},{64,32},{96,64},{1,97},{33,1},{65,33},{97,65},{2,98}... | collective-permute-start | bytes 1572872 | tf_op jit(solution)/shard_map/ppermute | solution.py:33
  85.6 25.3 %collective-permute-done = bf16[8,2,64,256]{3,2,1,0:T(8,128)(2,1)} collective-permute-done((bf16[8,2,64,256]{3,2,1,0:T(8,128)(2,1)}, bf16[8,2,64,256]{3,2,1,0:T(8,128)(2,1)}, u32[]{:S(2)}, u32[]{:S(2)}) %collective-permute-start) | collective-permute-done | bytes 524320 | tf_op jit(solution)/shard_map/ppermute | solution.py:33
  110.9 5.6 %collective-permute-done.1 = bf16[8,2,64,256]{3,2,1,0:T(8,128)(2,1)} collective-permute-done((bf16[8,2,64,256]{3,2,1,0:T(8,128)(2,1)}, bf16[8,2,64,256]{3,2,1,0:T(8,128)(2,1)}, u32[]{:S(2)}, u32[]{:S(2)}) %collective-permute-start.1) | collective-permute-done | bytes 524320 | tf_op jit(solution)/shard_map/ppermute | solution.py:33
  116.5 3.9 %collective-permute-done.2 = bf16[8,2,64,256]{3,2,1,0:T(8,128)(2,1)} collective-permute-done((bf16[8,2,64,256]{3,2,1,0:T(8,128)(2,1)}, bf16[8,2,64,256]{3,2,1,0:T(8,128)(2,1)}, u32[]{:S(2)}, u32[]{:S(2)}) %collective-permute-start.2) | collective-permute-done | bytes 524320 | tf_op jit(solution)/shard_map/ppermute | solution.py:33
  120.4 3.1 %pad_maximum_fusion.1 = bf16[4,8,2,64,256]{4,3,2,1,0:T(8,128)(2,1)} fusion(bf16[1,8,2,64,256]{4,3,2,1,0:T(8,128)(2,1)} %bitcast.12, bf16[1,8,2,64,256]{4,3,2,1,0:T(8,128)(2,1)} %bitcast.11, bf16[1,8,2,64,256]{4,3,2,1,0:T(8,128)(2,1)} %bitcast.10, bf16[1,8,2,64,256]{4,3,2,1,0:T(8,128)(2,1)} %bitcast.8), kind=kLoop, calls=%fused_computation.9 | loop fusion | flops 3145728 | bytes 4194304 | tf_op jit(solution)/shard_map/stack | solution.py:34
  123.5 3.6 %gather_fusion = bf16[4,8,2,64,256]{4,3,2,1,0:T(8,128)(2,1)} fusion(bf16[4,8,2,64,256]{4,3,2,1,0:T(8,128)(2,1)} %pad_maximum_fusion.1, s32[1024]{0:T(1024)S(1)} %pad_clamp_fusion.1), kind=kCustom, calls=%fused_computation | custom fusion | bytes 4194320 | tf_op jit(solution)/shard_map/jit(_take)/gather | solution.py:35
  127.1 3.2 %broadcast_select_fusion = bf16[4,8,2,64,256]{4,3,2,1,0:T(8,128)(2,1)} fusion(bf16[4,8,2,64,256]{4,3,2,1,0:T(8,128)(2,1)} %gather_fusion, pred[4]{0:T(512)(128)(4,1)S(1)} %compare_and_fusion), kind=kLoop, calls=%fused_computation.11 | loop fusion | flops 1048576 | bytes 4194308 | tf_op jit(solution)/shard_map/jit(_take)/select_n | solution.py:35
  130.3 1.9 %collective-permute-start.3 = (bf16[4,8,2,64,256]{4,3,2,1,0:T(8,128)(2,1)}, bf16[4,8,2,64,256]{4,3,2,1,0:T(8,128)(2,1)}, u32[]{:S(2)}, u32[]{:S(2)}) collective-permute-start(bf16[4,8,2,64,256]{4,3,2,1,0:T(8,128)(2,1)} %broadcast_select_fusion), channel_id=1, source_target_pairs={{0,8},{8,0},{1,9},{9,1},{2,10},{10,2},{3,11},{11,3},{4,12},{12,4},... | collective-permute-start | bytes 6291464 | tf_op jit(solution)/shard_map/ppermute | solution.py:33
  132.3 0.1 copy.47
  132.3 0.0 copy-start.4
  132.4 0.1 iota_compare_fusion
  132.5 0.6 copy-done.4
  133.1 2.9 %fusion.31 = (f32[4,48,8]{2,0,1:T(4,128)S(1)}, f32[4,48,1,8,96]{4,3,0,1,2:T(8,128)}) fusion(bf16[48,1,2,96,128]{4,3,2,1,0:T(8,128)(2,1)} %param.9, pred[48,96]{1,0:T(8,128)(4,1)S(1)} %iota_compare_fusion, bf16[4,48,8,128]{3,2,1,0:T(8,128)(2,1)S(1)} %bitcast.126), kind=kOutput, calls=%fused_computation.77 | convolution fusion | flops 38189568 | bytes 2173440 | tf_op jit(solution)/shard_map/srgpe,rgce->srgpc/dot_general | solution.py:63
  136.0 0.3 bitcast_select_fusion
  136.3 0.4 collective-permute-done.3
  136.7 4.0 %fusion.1 = (bf16[2,4,8,2,64,128]{5,4,3,2,1,0:T(8,128)(2,1)}, bf16[2,4,8,2,64,128]{5,4,3,2,1,0:T(8,128)(2,1)}) fusion(bf16[1,4,8,2,64,256]{5,4,3,2,1,0:T(8,128)(2,1)S(1)} %bitcast_select_fusion, bf16[1,4,8,2,64,256]{5,4,3,2,1,0:T(8,128)(2,1)} %bitcast.15), kind=kLoop, calls=%fused_computation.7 | loop fusion | flops 8388608 | bytes 8388608 | tf_op jit(solution)/shard_map/stack | solution.py:34
  140.7 3.8 %gather_fusion.1 = bf16[2,4,8,2,64,128]{5,4,3,2,1,0:T(8,128)(2,1)} fusion(bf16[2,4,8,2,64,128]{5,4,3,2,1,0:T(8,128)(2,1)} %get-tuple-element.5, s32[1024]{0:T(1024)S(1)} %pad_clamp_fusion), kind=kCustom, calls=%fused_computation.1 | custom fusion | bytes 4194312 | tf_op jit(solution)/shard_map/jit(_take)/gather | solution.py:35
  144.5 3.7 %gather_fusion.2 = bf16[2,4,8,2,64,128]{5,4,3,2,1,0:T(8,128)(2,1)} fusion(bf16[2,4,8,2,64,128]{5,4,3,2,1,0:T(8,128)(2,1)} %get-tuple-element.6, s32[1024]{0:T(1024)S(1)} %pad_clamp_fusion), kind=kCustom, calls=%fused_computation.2 | custom fusion | bytes 4194312 | tf_op jit(solution)/shard_map/jit(_take)/gather | solution.py:35
  148.2 3.2 %fusion = bf16[8,4,2,2,64,256]{5,4,2,0,1,3:T(8,128)(2,1)S(1)} fusion(bf16[2,4,8,2,64,128]{5,4,3,2,1,0:T(8,128)(2,1)} %gather_fusion.2, bf16[2,4,8,2,64,128]{5,4,3,2,1,0:T(8,128)(2,1)} %gather_fusion.1, pred[2]{0:T(512)(128)(4,1)S(1)} %compare_and_fusion.1), kind=kLoop, calls=%fused_computation.6 | loop fusion | flops 10485760 | bytes 8388610 | tf_op jit(solution)/shard_map/jit(_take)/select_n | solution.py:35
  151.4 0.6 copy.31
  152.0 0.0 copy-done
  152.0 1.1 fusion.13
  153.2 0.0 copy-start.2
  153.2 0.1 fusion.30
  153.3 2.9 %fusion.32 = (f32[4,48,8]{2,0,1:T(4,128)S(1)}, f32[4,48,1,8,4]{3,4,0,1,2:T(4,128)S(1)}) fusion(bf16[4,48,1,1,128]{4,3,1,0,2:T(2,128)(2,1)S(1)} %get-tuple-element.8, pred[4,4]{1,0:T(4,128)(4,1)S(1)} %iota_compare_fusion.1, bf16[4,48,8,128]{3,2,1,0:T(8,128)(2,1)} %bitcast.127), kind=kOutput, calls=%fused_computation.78 | convolution fusion | flops 1589760 | bytes 473104 | tf_op jit(solution)/shard_map/srgpe,trge->srgpt/dot_general | solution.py:70
  156.3 0.4 fusion.20
  156.7 0.0 copy-start.7
  156.7 0.6 fusion.15
  157.3 0.4 fusion.21
  157.7 0.6 copy-done.7
  158.3 0.6 fusion.7
  158.9 0.8 reshape.263
  159.8 3.5 %all-to-all-start.1 = ((bf16[4,48,1024]{2,0,1:T(4,128)(2,1)}), bf16[4,48,1024]{2,0,1:T(4,128)(2,1)S(1)}, u32[]{:S(2)}, u32[]{:S(2)}) async-start(bf16[4,48,1024]{2,0,1:T(4,128)(2,1)} %reshape.263), calls=%async_computation.1 | async-start | bytes 786432 | tf_op jit(solution)/shard_map/all_to_all | solution.py:91
  163.3 0.6 convert_element_type.56
  163.9 8.6 %all-to-all-done.1 = bf16[4,48,1024]{2,0,1:T(4,128)(2,1)S(1)} async-done(((bf16[4,48,1024]{2,0,1:T(4,128)(2,1)}), bf16[4,48,1024]{2,0,1:T(4,128)(2,1)S(1)}, u32[]{:S(2)}, u32[]{:S(2)}) %all-to-all-start.1) | async-done | bytes 393248 | tf_op jit(solution)/shard_map/all_to_all | solution.py:91
  172.4 1.1 copy.63
  173.6 2.5 %reshape.264 = f32[4,6,8192]{2,0,1:T(4,128)} reshape(f32[4,6,8,1024]{3,2,0,1:T(8,128)} %bitcast.124) | data formatting | bytes 1572864 | tf_op jit(solution)/shard_map/convert_element_type | solution.py:92
  176.1 0.9 multiply_reduce_fusion
  177.0 0.8 copy.37
  177.8 0.1 reduce_sum.37
  177.9 0.1 copy.38
  178.0 2.1 %multiply_convert_fusion = bf16[4,6,8192]{2,0,1:T(4,128)(2,1)} fusion(f32[4,6,8192]{2,0,1:T(4,128)} %reshape.264, f32[8192]{0:T(1024)} %convert_element_type.56, f32[4,6]{0,1:T(8,128)S(1)} %copy.38), kind=kLoop, calls=%fused_computation.30 | loop fusion | flops 589824 | bytes 1212512 | tf_op jit(solution)/shard_map/convert_element_type | solution.py:95
  (21 shorter events, 0.2 us)
Async XLA Ops:
  0.0 152.0 %copy-start = (bf16[4,48,8192]{2,1,0:T(8,128)(2,1)S(1)}, bf16[4,48,8192]{2,1,0:T(8,128)(2,1)}, u32[]{:S(2)}) copy-start(bf16[4,48,8192]{2,1,0:T(8,128)(2,1)} %param.6) | copy-start | bytes 9437188
  75.4 35.5 %collective-permute-start = (bf16[8,2,64,256]{3,2,1,0:T(8,128)(2,1)}, bf16[8,2,64,256]{3,2,1,0:T(8,128)(2,1)}, u32[]{:S(2)}, u32[]{:S(2)}) collective-permute-start(bf16[8,2,64,256]{3,2,1,0:T(8,128)(2,1)} %bitcast.9), channel_id=1, source_target_pairs={{0,32},{32,64},{64,96},{96,0},{1,33},{33,65},{65,97},{97,1},{2,34}... | collective-permute-start | bytes 1572872 | tf_op jit(solution)/shard_map/ppermute | solution.py:33
  77.5 39.0 %collective-permute-start.1 = (bf16[8,2,64,256]{3,2,1,0:T(8,128)(2,1)}, bf16[8,2,64,256]{3,2,1,0:T(8,128)(2,1)}, u32[]{:S(2)}, u32[]{:S(2)}) collective-permute-start(bf16[8,2,64,256]{3,2,1,0:T(8,128)(2,1)} %bitcast.9), channel_id=1, source_target_pairs={{0,64},{32,96},{64,0},{96,32},{1,65},{33,97},{65,1},{97,33},{2,66}... | collective-permute-start | bytes 1572872 | tf_op jit(solution)/shard_map/ppermute | solution.py:33
  83.7 36.7 %collective-permute-start.2 = (bf16[8,2,64,256]{3,2,1,0:T(8,128)(2,1)}, bf16[8,2,64,256]{3,2,1,0:T(8,128)(2,1)}, u32[]{:S(2)}, u32[]{:S(2)}) collective-permute-start(bf16[8,2,64,256]{3,2,1,0:T(8,128)(2,1)} %bitcast.9), channel_id=1, source_target_pairs={{0,96},{32,0},{64,32},{96,64},{1,97},{33,1},{65,33},{97,65},{2,98}... | collective-permute-start | bytes 1572872 | tf_op jit(solution)/shard_map/ppermute | solution.py:33
  127.1 5.2 %copy-start.3 = (bf16[4,48,1024]{2,1,0:T(8,128)(2,1)S(1)}, bf16[4,48,1024]{2,1,0:T(8,128)(2,1)}, u32[]{:S(2)}) copy-start(bf16[4,48,1024]{2,1,0:T(8,128)(2,1)} %param.8) | copy-start | bytes 1179652
  127.1 5.3 %copy-start.6 = (s32[48]{0:T(128)S(1)}, s32[48]{0:T(128)}, u32[]{:S(2)}) copy-start(s32[48]{0:T(128)} %param.10) | copy-start | bytes 580
  130.3 6.4 %collective-permute-start.3 = (bf16[4,8,2,64,256]{4,3,2,1,0:T(8,128)(2,1)}, bf16[4,8,2,64,256]{4,3,2,1,0:T(8,128)(2,1)}, u32[]{:S(2)}, u32[]{:S(2)}) collective-permute-start(bf16[4,8,2,64,256]{4,3,2,1,0:T(8,128)(2,1)} %broadcast_select_fusion), channel_id=1, source_target_pairs={{0,8},{8,0},{1,9},{9,1},{2,10},{10,2},{3,11},{11,3},{4,12},{12,4},... | collective-permute-start | bytes 6291464 | tf_op jit(solution)/shard_map/ppermute | solution.py:33
  132.2 3.8 %copy-start.1 = (bf16[4,8,2,64,256]{4,3,2,1,0:T(8,128)(2,1)S(1)}, bf16[4,8,2,64,256]{4,3,2,1,0:T(8,128)(2,1)}, u32[]{:S(2)}) copy-start(bf16[4,8,2,64,256]{4,3,2,1,0:T(8,128)(2,1)} %gather_fusion) | copy-start | bytes 6291460
  132.3 0.7 copy-start.4
  153.2 3.5 %copy-start.2 = (f32[4,48,1,8,96]{4,3,0,1,2:T(8,128)S(1)}, f32[4,48,1,8,96]{4,3,0,1,2:T(8,128)}, u32[]{:S(2)}) copy-start(f32[4,48,1,8,96]{4,3,0,1,2:T(8,128)} %get-tuple-element.10) | copy-start | bytes 1769476
  156.7 1.7 copy-start.7
  158.3 4.9 %copy-start.5 = (bf16[8192]{0:T(1024)(128)(2,1)S(1)}, bf16[8192]{0:T(1024)(128)(2,1)}, u32[]{:S(2)}) copy-start(bf16[8192]{0:T(1024)(128)(2,1)} %param.11) | copy-start | bytes 49156
  159.8 12.7 %all-to-all-start.1 = ((bf16[4,48,1024]{2,0,1:T(4,128)(2,1)}), bf16[4,48,1024]{2,0,1:T(4,128)(2,1)S(1)}, u32[]{:S(2)}, u32[]{:S(2)}) async-start(bf16[4,48,1024]{2,0,1:T(4,128)(2,1)} %reshape.263), calls=%async_computation.1 | async-start | bytes 786432 | tf_op jit(solution)/shard_map/all_to_all | solution.py:91

commit v3 on v2

--- a/solution.py
+++ b/solution.py
@@ -29,10 +29,8 @@
 
 
 def pp_gather(x, axis, n):
-    me = lax.axis_index(axis)
-    pieces = [x] + [lax.ppermute(x, axis, [(k, (k + d) % n) for k in range(n)]) for d in range(1, n)]
-    rel = jnp.stack(pieces)
-    return jnp.take(rel, (me - jnp.arange(n)) % n, axis=0)
+    spread = jnp.broadcast_to(x[None], (n,) + x.shape)
+    return lax.all_to_all(spread, axis, 0, 0, tiled=True)
 
 
 def gather_w(own_piece, zb_pp, core_pp):

time: 181 us -> 163 us (0.901)
  the two profiles are of different devices: /device:TPU:32 before, /device:TPU:1 now
where the time goes in v3:
time: 163 us; the launch traced here: 162 us
  blocking collectives  78.7 us (48%)
  waiting for transfers between devices  51.4 us (32%)
  local copies, waits for them, and re-layouts  11.4 us (7%)
  starting transfers between devices  8.02 us (5%)
  matrix products  7.97 us (5%)
  other arithmetic  4.75 us (3%)
    all_gather x1, blocking collectives, gather_w(): t = lax.all_gather(t, 'dp_0a')  54.2 us
    all_to_all x1, waiting for transfers between devices, pp_gather(): return lax.all_to_all(spread, axis, 0, 0, tiled=True)  43.8 us
    all_to_all x1, blocking collectives, per_device(): lax.all_to_all(kv_weight, 'tp', split_axis=1, concat_axis=0, tiled=True)  11.3 us
    all_to_all x1, blocking collectives, pp_gather(): return lax.all_to_all(spread, axis, 0, 0, tiled=True)  8.36 us
    all_to_all x1, waiting for transfers between devices, per_device(): lax.all_to_all(attn, 'tp', split_axis=1, concat_axis=2, tiled=True)  7.56 us
    all_gather x1, blocking collectives, gather_w(): t = lax.all_gather(own_piece, 'dp_1')  4.92 us
    all_to_all x1, starting transfers between devices, pp_gather(): return lax.all_to_all(spread, axis, 0, 0, tiled=True)  4.57 us
    convert_element_type x2, local copies, waits for them, and re-layouts, per_device(): values = arrived.astype(jnp.float32)  3.67 us
  transfers between devices with their start and end apart: 2, of which 2 were waited for; matrix products, arithmetic and copies ran while one was open for 2% of the time, Pallas kernels for 0%

profile of v3, /device:TPU:1, one launch (start us, length us, event | category | flops | bytes accessed | tf_op | source)
XLA Modules:
  0.0 162.5 jit_solution(10465562900808110414)
XLA Ops:
  0.0 0.0 copy-start
  0.0 11.3 %all_to_all.35 = bf16[8,8,256]{2,0,1:T(8,128)(2,1)S(1)} all-to-all(bf16[8,8,256]{2,0,1:T(8,128)(2,1)} %bitcast.117), channel_id=1, replica_groups=mesh['dp_0a'=8,'dp_0b'=4,'dp_1'=2,'dp_2'=2,'tp'=8] {'tp'}, dimensions={1} | all-to-all | bytes 65536 | tf_op jit(solution)/shard_map/all_to_all | solution.py:47
  11.3 4.9 %all_gather.13 = bf16[2,64,256]{2,1,0:T(8,128)(2,1)S(1)} all-gather(bf16[1,64,256]{2,1,0:T(8,128)(2,1)S(1)} %bitcast.116), channel_id=1, replica_groups=mesh['dp_0a'=8,'dp_0b'=4,'dp_1'=2,'dp_2'=2,'tp'=8] {'dp_1'}, dimensions={0}, use_global_device_ids=true | all-gather | bytes 98304 | tf_op jit(solution)/shard_map/all_gather | solution.py:37
  16.2 54.2 %all-gather = bf16[16,64,256]{2,1,0:T(8,128)(2,1)S(1)} all-gather(bf16[2,64,256]{2,1,0:T(8,128)(2,1)S(1)} %all_gather.13), channel_id=2, replica_groups=mesh['dp_0a'=8,'dp_0b'=4,'dp_1'=2,'dp_2'=2,'tp'=8] {'dp_0a'}, dimensions={0}, use_global_device_ids=true | all-gather | bytes 589824 | tf_op jit(solution)/shard_map/all_gather | solution.py:38
  70.4 1.6 broadcast_in_dim.31
  71.9 0.0 copy-start.2
  71.9 0.0 copy-start.5
  71.9 4.6 %all-to-all-start.1 = ((bf16[4,8,2,64,256]{4,3,2,1,0:T(8,128)(2,1)}), bf16[4,8,2,64,256]{4,3,2,1,0:T(8,128)(2,1)}, u32[]{:S(2)}, u32[]{:S(2)}) async-start(bf16[4,8,2,64,256]{4,3,2,1,0:T(8,128)(2,1)} %broadcast_in_dim.31), calls=%async_computation.1 | async-start | bytes 4194304 | tf_op jit(solution)/shard_map/all_to_all | solution.py:33
  76.5 0.0 copy-done.2
  76.5 0.1 copy.40
  76.6 0.0 copy-start.3
  76.6 0.0 copy-done.5
  76.6 0.1 iota_compare_fusion
  76.7 0.6 copy-done.3
  77.4 2.9 %fusion.22 = (f32[4,48,8]{2,0,1:T(4,128)S(1)}, f32[4,48,1,8,96]{4,3,0,1,2:T(8,128)}) fusion(bf16[48,1,2,96,128]{4,3,2,1,0:T(8,128)(2,1)} %param.9, pred[48,96]{1,0:T(8,128)(4,1)S(1)} %iota_compare_fusion, bf16[4,48,8,128]{3,2,1,0:T(8,128)(2,1)S(1)} %bitcast.114), kind=kOutput, calls=%fused_computation.38 | convolution fusion | flops 38189568 | bytes 2173440 | tf_op jit(solution)/shard_map/srgpe,rgce->srgpc/dot_general | solution.py:61
  80.3 43.8 %all-to-all-done.1 = bf16[4,8,2,64,256]{4,3,2,1,0:T(8,128)(2,1)} async-done(((bf16[4,8,2,64,256]{4,3,2,1,0:T(8,128)(2,1)}), bf16[4,8,2,64,256]{4,3,2,1,0:T(8,128)(2,1)}, u32[]{:S(2)}, u32[]{:S(2)}) %all-to-all-start.1) | async-done | bytes 2097184 | tf_op jit(solution)/shard_map/all_to_all | solution.py:33
  124.1 1.7 %copy.23 = bf16[4,8,2,64,256]{4,3,2,0,1:T(8,128)(2,1)S(1)} copy(bf16[4,8,2,64,256]{4,3,2,1,0:T(8,128)(2,1)} %all-to-all-done.1) | data formatting | bytes 4194304 | tf_op jit(solution)/shard_map/all_to_all | solution.py:33
  125.8 0.5 broadcast_in_dim.32
  126.4 8.4 %all_to_all.36 = bf16[2,4,8,2,64,256]{5,4,3,1,2,0:T(8,128)(2,1)S(1)} all-to-all(bf16[2,4,8,2,64,256]{5,4,3,1,2,0:T(8,128)(2,1)S(1)} %broadcast_in_dim.32), channel_id=1, replica_groups=mesh['dp_0a'=8,'dp_0b'=4,'dp_1'=2,'dp_2'=2,'tp'=8] {'dp_2'}, dimensions={0} | all-to-all | bytes 8388608 | tf_op jit(solution)/shard_map/all_to_all | solution.py:33
  134.7 0.6 copy.24
  135.3 0.0 copy-done
  135.3 1.1 convolution_convert_fusion
  136.5 0.0 copy-start.1
  136.5 0.1 fusion.21
  136.6 2.9 %fusion.23 = (f32[4,48,8]{2,0,1:T(4,128)S(1)}, f32[4,48,1,8,4]{3,4,0,1,2:T(4,128)S(1)}) fusion(bf16[4,48,1,1,128]{4,3,1,0,2:T(2,128)(2,1)S(1)} %get-tuple-element.6, pred[4,4]{1,0:T(4,128)(4,1)S(1)} %iota_compare_fusion.1, bf16[4,48,8,128]{3,2,1,0:T(8,128)(2,1)} %bitcast.115), kind=kOutput, calls=%fused_computation.39 | convolution fusion | flops 1589760 | bytes 473104 | tf_op jit(solution)/shard_map/srgpe,trge->srgpt/dot_general | solution.py:68
  139.6 0.4 fusion.17
  140.0 0.0 copy-start.6
  140.0 0.0 copy-done.1
  140.0 0.6 fusion.12
  140.6 0.4 fusion.18
  141.0 0.6 copy-done.6
  141.7 0.0 copy-start.4
  141.7 0.6 fusion.5
  142.3 0.8 reshape.150
  143.1 3.5 %all-to-all-start.3 = ((bf16[4,48,1024]{2,0,1:T(4,128)(2,1)}), bf16[4,48,1024]{2,0,1:T(4,128)(2,1)S(1)}, u32[]{:S(2)}, u32[]{:S(2)}) async-start(bf16[4,48,1024]{2,0,1:T(4,128)(2,1)} %reshape.150), calls=%async_computation.3 | async-start | bytes 786432 | tf_op jit(solution)/shard_map/all_to_all | solution.py:89
  146.6 0.0 copy-done.4
  146.6 0.6 convert_element_type.52
  147.2 7.6 %all-to-all-done.3 = bf16[4,48,1024]{2,0,1:T(4,128)(2,1)S(1)} async-done(((bf16[4,48,1024]{2,0,1:T(4,128)(2,1)}), bf16[4,48,1024]{2,0,1:T(4,128)(2,1)S(1)}, u32[]{:S(2)}, u32[]{:S(2)}) %all-to-all-start.3) | async-done | bytes 393248 | tf_op jit(solution)/shard_map/all_to_all | solution.py:89
  154.7 1.1 copy.56
  155.9 2.5 %reshape.151 = f32[4,6,8192]{2,0,1:T(4,128)} reshape(f32[4,6,8,1024]{3,2,0,1:T(8,128)} %bitcast.111) | data formatting | bytes 1572864 | tf_op jit(solution)/shard_map/convert_element_type | solution.py:90
  158.4 0.9 multiply_reduce_fusion
  159.3 0.8 copy.30
  160.1 0.1 reduce_sum.37
  160.2 0.1 copy.31
  160.3 2.1 %multiply_convert_fusion = bf16[4,6,8192]{2,0,1:T(4,128)(2,1)} fusion(f32[4,6,8192]{2,0,1:T(4,128)} %reshape.151, f32[8192]{0:T(1024)} %convert_element_type.52, f32[4,6]{0,1:T(8,128)S(1)} %copy.31), kind=kLoop, calls=%fused_computation.17 | loop fusion | flops 589824 | bytes 1212512 | tf_op jit(solution)/shard_map/convert_element_type | solution.py:93
  (6 shorter events, 0.1 us)
Async XLA Ops:
  0.0 135.3 %copy-start = (bf16[4,48,8192]{2,1,0:T(8,128)(2,1)S(1)}, bf16[4,48,8192]{2,1,0:T(8,128)(2,1)}, u32[]{:S(2)}) copy-start(bf16[4,48,8192]{2,1,0:T(8,128)(2,1)} %param.6) | copy-start | bytes 9437188
  71.9 4.6 %copy-start.2 = (bf16[4,48,1024]{2,1,0:T(8,128)(2,1)S(1)}, bf16[4,48,1024]{2,1,0:T(8,128)(2,1)}, u32[]{:S(2)}) copy-start(bf16[4,48,1024]{2,1,0:T(8,128)(2,1)} %param.8) | copy-start | bytes 1179652
  71.9 4.7 %copy-start.5 = (s32[48]{0:T(128)S(1)}, s32[48]{0:T(128)}, u32[]{:S(2)}) copy-start(s32[48]{0:T(128)} %param.10) | copy-start | bytes 580
  71.9 52.2 %all-to-all-start.1 = ((bf16[4,8,2,64,256]{4,3,2,1,0:T(8,128)(2,1)}), bf16[4,8,2,64,256]{4,3,2,1,0:T(8,128)(2,1)}, u32[]{:S(2)}, u32[]{:S(2)}) async-start(bf16[4,8,2,64,256]{4,3,2,1,0:T(8,128)(2,1)} %broadcast_in_dim.31), calls=%async_computation.1 | async-start | bytes 4194304 | tf_op jit(solution)/shard_map/all_to_all | solution.py:33
  76.6 0.7 copy-start.3
  136.5 3.5 %copy-start.1 = (f32[4,48,1,8,96]{4,3,0,1,2:T(8,128)S(1)}, f32[4,48,1,8,96]{4,3,0,1,2:T(8,128)}, u32[]{:S(2)}) copy-start(f32[4,48,1,8,96]{4,3,0,1,2:T(8,128)} %get-tuple-element.8) | copy-start | bytes 1769476
  140.0 1.7 %copy-start.6 = (bf16[48,1,2,96,128]{4,3,2,1,0:T(8,128)(2,1)S(1)}, bf16[48,1,2,96,128]{4,3,2,1,0:T(8,128)(2,1)}, u32[]{:S(2)}) copy-start(bf16[48,1,2,96,128]{4,3,2,1,0:T(8,128)(2,1)} %param.9) | copy-start | bytes 7077892
  141.7 4.9 %copy-start.4 = (bf16[8192]{0:T(1024)(128)(2,1)S(1)}, bf16[8192]{0:T(1024)(128)(2,1)}, u32[]{:S(2)}) copy-start(bf16[8192]{0:T(1024)(128)(2,1)} %param.11) | copy-start | bytes 49156
  143.1 11.6 %all-to-all-start.3 = ((bf16[4,48,1024]{2,0,1:T(4,128)(2,1)}), bf16[4,48,1024]{2,0,1:T(4,128)(2,1)S(1)}, u32[]{:S(2)}, u32[]{:S(2)}) async-start(bf16[4,48,1024]{2,0,1:T(4,128)(2,1)} %reshape.150), calls=%async_computation.3 | async-start | bytes 786432 | tf_op jit(solution)/shard_map/all_to_all | solution.py:89

commit v4 on v3

--- a/solution.py
+++ b/solution.py
@@ -33,21 +33,23 @@
     return lax.all_to_all(spread, axis, 0, 0, tiled=True)
 
 
-def gather_w(own_piece, zb_pp, core_pp):
-    t = lax.all_gather(own_piece, "dp_1")
+def gather_w(kv_weight, groups):
+    rows, width = kv_weight.shape
+    cols = width // groups
+    mine = kv_weight.reshape(rows, groups, cols).transpose(1, 0, 2)
+    spread = jnp.broadcast_to(mine[None], (2,) + mine.shape).reshape(2 * groups, rows, cols)
+    t = lax.all_to_all(spread, ("dp_1", "tp"), 0, 0, tiled=True).reshape(2, groups, rows, cols)
     t = lax.all_gather(t, "dp_0a")
-    t = pp_gather(t, "dp_0b", 4) if zb_pp else lax.all_gather(t, "dp_0b")
-    t = pp_gather(t, "dp_2", 2) if core_pp else lax.all_gather(t, "dp_2")
-    return t.transpose(2, 1, 3, 0, 4, 5).reshape(-1, own_piece.shape[1])
-
+    t = pp_gather(t, "dp_0b", 4)
+    t = pp_gather(t, "dp_2", 2)
+    return t.transpose(2, 1, 3, 0, 4, 5, 6).reshape(-1, cols)
 
 def per_device(hidden, kv_weight, queries, kv_cache, lengths, out_gain):
     steps, rows, width = hidden.shape
     local_groups = kv_cache.shape[1]
-    own_piece = lax.all_to_all(kv_weight, "tp", split_axis=1, concat_axis=0, tiled=True)
     flat_rows = hidden.reshape(steps * rows, width)
     projected = jnp.dot(
-        flat_rows, gather_w(own_piece, True, True), preferred_element_type=jnp.float32
+        flat_rows, gather_w(kv_weight, kv_weight.shape[1] // (2 * kv_cache.shape[4])), preferred_element_type=jnp.float32
     )
     head_size = kv_cache.shape[4]
     fresh = projected.astype(jnp.bfloat16).reshape(steps, rows, local_groups, 2, head_size)

time: 163 us -> 159 us (0.975)
  blocking collectives: 78.7 us -> 74.4 us
    all_gather x1 -> x0, blocking collectives: 4.92 us -> none  [gather_w(): t = lax.all_gather(own_piece, 'dp_1')]
    all_to_all x1, blocking collectives: 11.3 us -> 14 us  [gather_w(): lax.all_to_all(spread, ('dp_1', 'tp'), 0, 0, tiled=True)]
    all_gather x1, blocking collectives: 54.2 us -> 51.9 us  [gather_w(): t = lax.all_gather(t, 'dp_0a')]
where the time goes in v4:
time: 159 us
  blocking collectives  74.4 us (47%)
  waiting for transfers between devices  51.2 us (32%)
  local copies, waits for them, and re-layouts  12.3 us (8%)
  starting transfers between devices  8.02 us (5%)
  matrix products  7.96 us (5%)
  other arithmetic  4.75 us (3%)
    all_gather x1, blocking collectives, gather_w(): t = lax.all_gather(t, 'dp_0a')  51.9 us
    all_to_all x1, waiting for transfers between devices, pp_gather(): return lax.all_to_all(spread, axis, 0, 0, tiled=True)  43.7 us
    all_to_all x1, blocking collectives, gather_w(): lax.all_to_all(spread, ('dp_1', 'tp'), 0, 0, tiled=True)  14 us
    all_to_all x1, blocking collectives, pp_gather(): return lax.all_to_all(spread, axis, 0, 0, tiled=True)  8.52 us
    all_to_all x1, waiting for transfers between devices, per_device(): lax.all_to_all(attn, 'tp', split_axis=1, concat_axis=2, tiled=True)  7.56 us
    all_to_all x1, starting transfers between devices, pp_gather(): return lax.all_to_all(spread, axis, 0, 0, tiled=True)  4.57 us
    convert_element_type x2, local copies, waits for them, and re-layouts, per_device(): values = arrived.astype(jnp.float32)  3.67 us
    all_to_all x1, starting transfers between devices, per_device(): lax.all_to_all(attn, 'tp', split_axis=1, concat_axis=2, tiled=True)  3.45 us
  transfers between devices with their start and end apart: 2, of which 2 were waited for; matrix products, arithmetic and copies ran while one was open for 2% of the time, Pallas kernels for 0%

profile of v4, /device:TPU:1, one launch (start us, length us, event | category | flops | bytes accessed | tf_op | source)
XLA Modules:
  0.0 158.9 jit_solution(11675727635667052736)
XLA Ops:
  0.0 0.0 copy-start
  0.0 0.9 broadcast_in_dim.29
  0.9 14.0 %all_to_all.24 = bf16[16,8,256]{2,1,0:T(8,128)(2,1)S(1)} all-to-all(bf16[16,8,256]{2,1,0:T(8,128)(2,1)S(1)} %bitcast.116), channel_id=1, replica_groups=mesh['dp_0a'=8,'dp_0b'=4,'dp_1'=2,'dp_2'=2,'tp'=8] {'dp_1','tp'}, dimensions={0} | all-to-all | bytes 131072 | tf_op jit(solution)/shard_map/all_to_all | solution.py:41
  14.9 51.9 %all_gather.3 = bf16[8,2,8,8,256]{4,3,2,1,0:T(8,128)(2,1)S(1)} all-gather(bf16[1,2,8,8,256]{4,3,2,1,0:T(8,128)(2,1)S(1)} %bitcast.115), channel_id=1, replica_groups=mesh['dp_0a'=8,'dp_0b'=4,'dp_1'=2,'dp_2'=2,'tp'=8] {'dp_0a'}, dimensions={0}, use_global_device_ids=true | all-gather | bytes 589824 | tf_op jit(solution)/shard_map/all_gather | solution.py:42
  66.8 1.6 broadcast_in_dim.34
  68.4 0.0 copy-start.2
  68.4 0.0 copy-start.5
  68.4 4.6 %all-to-all-start.1 = ((bf16[4,8,2,8,8,256]{5,4,3,2,1,0:T(8,128)(2,1)}), bf16[4,8,2,8,8,256]{5,4,3,2,1,0:T(8,128)(2,1)}, u32[]{:S(2)}, u32[]{:S(2)}) async-start(bf16[4,8,2,8,8,256]{5,4,3,2,1,0:T(8,128)(2,1)} %broadcast_in_dim.34), calls=%async_computation.1 | async-start | bytes 4194304 | tf_op jit(solution)/shard_map/all_to_all | solution.py:33
  72.9 0.0 copy-done.2
  72.9 0.1 copy.40
  73.0 0.0 copy-start.3
  73.0 0.0 copy-done.5
  73.1 0.1 iota_compare_fusion
  73.1 0.6 copy-done.3
  73.8 2.9 %fusion.22 = (f32[4,48,8]{2,0,1:T(4,128)S(1)}, f32[4,48,1,8,96]{4,3,0,1,2:T(8,128)}) fusion(bf16[48,1,2,96,128]{4,3,2,1,0:T(8,128)(2,1)} %param.9, pred[48,96]{1,0:T(8,128)(4,1)S(1)} %iota_compare_fusion, bf16[4,48,8,128]{3,2,1,0:T(8,128)(2,1)S(1)} %bitcast.113), kind=kOutput, calls=%fused_computation.38 | convolution fusion | flops 38189568 | bytes 2173440 | tf_op jit(solution)/shard_map/srgpe,rgce->srgpc/dot_general | solution.py:63
  76.7 43.7 %all-to-all-done.1 = bf16[4,8,2,8,8,256]{5,4,3,2,1,0:T(8,128)(2,1)} async-done(((bf16[4,8,2,8,8,256]{5,4,3,2,1,0:T(8,128)(2,1)}), bf16[4,8,2,8,8,256]{5,4,3,2,1,0:T(8,128)(2,1)}, u32[]{:S(2)}, u32[]{:S(2)}) %all-to-all-start.1) | async-done | bytes 2097184 | tf_op jit(solution)/shard_map/all_to_all | solution.py:33
  120.4 1.7 %copy.23 = bf16[4,8,2,8,8,256]{5,4,3,2,0,1:T(8,128)(2,1)S(1)} copy(bf16[4,8,2,8,8,256]{5,4,3,2,1,0:T(8,128)(2,1)} %all-to-all-done.1) | data formatting | bytes 4194304 | tf_op jit(solution)/shard_map/all_to_all | solution.py:33
  122.1 0.5 broadcast_in_dim.35
  122.6 8.5 %all_to_all.25 = bf16[2,4,8,2,8,8,256]{6,5,4,3,1,2,0:T(8,128)(2,1)S(1)} all-to-all(bf16[2,4,8,2,8,8,256]{6,5,4,3,1,2,0:T(8,128)(2,1)S(1)} %broadcast_in_dim.35), channel_id=1, replica_groups=mesh['dp_0a'=8,'dp_0b'=4,'dp_1'=2,'dp_2'=2,'tp'=8] {'dp_2'}, dimensions={0} | all-to-all | bytes 8388608 | tf_op jit(solution)/shard_map/all_to_all | solution.py:33
  131.2 0.6 copy.24
  131.7 0.0 copy-done
  131.8 1.1 convolution_convert_fusion
  132.9 0.0 copy-start.1
  132.9 0.1 fusion.21
  133.0 2.9 %fusion.23 = (f32[4,48,8]{2,0,1:T(4,128)S(1)}, f32[4,48,1,8,4]{3,4,0,1,2:T(4,128)S(1)}) fusion(bf16[4,48,1,1,128]{4,3,1,0,2:T(2,128)(2,1)S(1)} %get-tuple-element.6, pred[4,4]{1,0:T(4,128)(4,1)S(1)} %iota_compare_fusion.1, bf16[4,48,8,128]{3,2,1,0:T(8,128)(2,1)} %bitcast.114), kind=kOutput, calls=%fused_computation.39 | convolution fusion | flops 1589760 | bytes 473104 | tf_op jit(solution)/shard_map/srgpe,trge->srgpt/dot_general | solution.py:70
  136.0 0.4 fusion.17
  136.4 0.0 copy-start.6
  136.4 0.0 copy-done.1
  136.4 0.6 fusion.12
  137.0 0.4 fusion.18
  137.5 0.6 copy-done.6
  138.1 0.0 copy-start.4
  138.1 0.6 fusion.5
  138.7 0.8 reshape.155
  139.5 3.5 %all-to-all-start.3 = ((bf16[4,48,1024]{2,0,1:T(4,128)(2,1)}), bf16[4,48,1024]{2,0,1:T(4,128)(2,1)S(1)}, u32[]{:S(2)}, u32[]{:S(2)}) async-start(bf16[4,48,1024]{2,0,1:T(4,128)(2,1)} %reshape.155), calls=%async_computation.3 | async-start | bytes 786432 | tf_op jit(solution)/shard_map/all_to_all | solution.py:91
  143.0 0.0 copy-done.4
  143.0 0.6 convert_element_type.52
  143.6 7.6 %all-to-all-done.3 = bf16[4,48,1024]{2,0,1:T(4,128)(2,1)S(1)} async-done(((bf16[4,48,1024]{2,0,1:T(4,128)(2,1)}), bf16[4,48,1024]{2,0,1:T(4,128)(2,1)S(1)}, u32[]{:S(2)}, u32[]{:S(2)}) %all-to-all-start.3) | async-done | bytes 393248 | tf_op jit(solution)/shard_map/all_to_all | solution.py:91
  151.1 1.1 copy.56
  152.3 2.5 %reshape.156 = f32[4,6,8192]{2,0,1:T(4,128)} reshape(f32[4,6,8,1024]{3,2,0,1:T(8,128)} %bitcast.111) | data formatting | bytes 1572864 | tf_op jit(solution)/shard_map/convert_element_type | solution.py:92
  154.8 0.9 multiply_reduce_fusion
  155.7 0.8 copy.30
  156.5 0.1 reduce_sum.37
  156.6 0.1 copy.31
  156.7 2.1 %multiply_convert_fusion = bf16[4,6,8192]{2,0,1:T(4,128)(2,1)} fusion(f32[4,6,8192]{2,0,1:T(4,128)} %reshape.156, f32[8192]{0:T(1024)} %convert_element_type.52, f32[4,6]{0,1:T(8,128)S(1)} %copy.31), kind=kLoop, calls=%fused_computation.17 | loop fusion | flops 589824 | bytes 1212512 | tf_op jit(solution)/shard_map/convert_element_type | solution.py:95
  (6 shorter events, 0.1 us)
Async XLA Ops:
  0.0 131.7 %copy-start = (bf16[4,48,8192]{2,1,0:T(8,128)(2,1)S(1)}, bf16[4,48,8192]{2,1,0:T(8,128)(2,1)}, u32[]{:S(2)}) copy-start(bf16[4,48,8192]{2,1,0:T(8,128)(2,1)} %param.6) | copy-start | bytes 9437188
  68.4 4.6 %copy-start.2 = (bf16[4,48,1024]{2,1,0:T(8,128)(2,1)S(1)}, bf16[4,48,1024]{2,1,0:T(8,128)(2,1)}, u32[]{:S(2)}) copy-start(bf16[4,48,1024]{2,1,0:T(8,128)(2,1)} %param.8) | copy-start | bytes 1179652
  68.4 4.7 %copy-start.5 = (s32[48]{0:T(128)S(1)}, s32[48]{0:T(128)}, u32[]{:S(2)}) copy-start(s32[48]{0:T(128)} %param.10) | copy-start | bytes 580
  68.4 52.0 %all-to-all-start.1 = ((bf16[4,8,2,8,8,256]{5,4,3,2,1,0:T(8,128)(2,1)}), bf16[4,8,2,8,8,256]{5,4,3,2,1,0:T(8,128)(2,1)}, u32[]{:S(2)}, u32[]{:S(2)}) async-start(bf16[4,8,2,8,8,256]{5,4,3,2,1,0:T(8,128)(2,1)} %broadcast_in_dim.34), calls=%async_computation.1 | async-start | bytes 4194304 | tf_op jit(solution)/shard_map/all_to_all | solution.py:33
  73.0 0.7 copy-start.3
  132.9 3.5 %copy-start.1 = (f32[4,48,1,8,96]{4,3,0,1,2:T(8,128)S(1)}, f32[4,48,1,8,96]{4,3,0,1,2:T(8,128)}, u32[]{:S(2)}) copy-start(f32[4,48,1,8,96]{4,3,0,1,2:T(8,128)} %get-tuple-element.8) | copy-start | bytes 1769476
  136.4 1.7 %copy-start.6 = (bf16[48,1,2,96,128]{4,3,2,1,0:T(8,128)(2,1)S(1)}, bf16[48,1,2,96,128]{4,3,2,1,0:T(8,128)(2,1)}, u32[]{:S(2)}) copy-start(bf16[48,1,2,96,128]{4,3,2,1,0:T(8,128)(2,1)} %param.9) | copy-start | bytes 7077892
  138.1 4.9 %copy-start.4 = (bf16[8192]{0:T(1024)(128)(2,1)S(1)}, bf16[8192]{0:T(1024)(128)(2,1)}, u32[]{:S(2)}) copy-start(bf16[8192]{0:T(1024)(128)(2,1)} %param.11) | copy-start | bytes 49156
  139.5 11.6 %all-to-all-start.3 = ((bf16[4,48,1024]{2,0,1:T(4,128)(2,1)}), bf16[4,48,1024]{2,0,1:T(4,128)(2,1)S(1)}, u32[]{:S(2)}, u32[]{:S(2)}) async-start(bf16[4,48,1024]{2,0,1:T(4,128)(2,1)} %reshape.155), calls=%async_computation.3 | async-start | bytes 786432 | tf_op jit(solution)/shard_map/all_to_all | solution.py:91

commit v5 on v4

--- a/solution.py
+++ b/solution.py
@@ -88,11 +88,14 @@
         "srgpt,trge->srgpe", new_weights, fresh[:, :, :, 1], preferred_element_type=jnp.float32
     )
     attn = mixed.astype(jnp.bfloat16).reshape(steps, rows, local_groups * per_group * head_size)
-    arrived = lax.all_to_all(attn, "tp", split_axis=1, concat_axis=2, tiled=True)
+    parts = lax.psum(1, "tp")
+    blocks = attn.reshape(steps, parts, rows // parts, attn.shape[2])
+    arrived = lax.all_to_all(blocks, "tp", split_axis=1, concat_axis=1, tiled=True)
     values = arrived.astype(jnp.float32)
-    square_mean = jnp.mean(values * values, -1, keepdims=True)
-    normed = values * lax.rsqrt(square_mean + 1e-05) * out_gain.astype(jnp.float32)
-    return normed.astype(jnp.bfloat16)
+    square_mean = jnp.mean(values * values, (1, 3), keepdims=True)
+    gain = out_gain.astype(jnp.float32).reshape(1, parts, 1, attn.shape[2])
+    normed = (values * lax.rsqrt(square_mean + 1e-05) * gain).astype(jnp.bfloat16)
+    return normed.transpose(0, 2, 1, 3).reshape(steps, rows // parts, parts * attn.shape[2])
 
 
 def solution(mesh):

time: 159 us -> 154 us (0.969)
  local copies, waits for them, and re-layouts: 12.3 us -> 9.17 us
  other arithmetic: 4.75 us -> 2.45 us
    convert_element_type x2 -> x0, local copies, waits for them, and re-layouts: 3.67 us -> none  [per_device(): values = arrived.astype(jnp.float32)]
    convert_element_type x2 -> x0, other arithmetic: 2.74 us -> none  [the longest x1 2.14 us: per_device(): return normed.astype(jnp.bfloat16)]
where the time goes in v5:
time: 154 us; the launch traced here: 153 us
  blocking collectives  74.4 us (48%)
  waiting for transfers between devices  51.2 us (33%)
  local copies, waits for them, and re-layouts  9.17 us (6%)
  starting transfers between devices  8.02 us (5%)
  matrix products  7.96 us (5%)
  other arithmetic  2.45 us (2%)
    all_gather x1, blocking collectives, gather_w(): t = lax.all_gather(t, 'dp_0a')  51.9 us
    all_to_all x1, waiting for transfers between devices, pp_gather(): return lax.all_to_all(spread, axis, 0, 0, tiled=True)  43.7 us
    all_to_all x1, blocking collectives, gather_w(): lax.all_to_all(spread, ('dp_1', 'tp'), 0, 0, tiled=True)  14 us
    all_to_all x1, blocking collectives, pp_gather(): return lax.all_to_all(spread, axis, 0, 0, tiled=True)  8.52 us
    all_to_all x1, waiting for transfers between devices, per_device(): lax.all_to_all(blocks, 'tp', split_axis=1, concat_axis=1, tiled=True)  7.55 us
    all_to_all x1, starting transfers between devices, pp_gather(): return lax.all_to_all(spread, axis, 0, 0, tiled=True)  4.57 us
    all_to_all x1, starting transfers between devices, per_device(): lax.all_to_all(blocks, 'tp', split_axis=1, concat_axis=1, tiled=True)  3.45 us
  transfers between devices with their start and end apart: 2, of which 2 were waited for; matrix products, arithmetic and copies ran while one was open for 2% of the time, Pallas kernels for 0%

profile of v5, /device:TPU:1, one launch (start us, length us, event | category | flops | bytes accessed | tf_op | source)
XLA Modules:
  0.0 153.4 jit_solution(5993086486311140710)
XLA Ops:
  0.0 0.0 copy-start
  0.0 0.9 broadcast_in_dim.29
  0.9 14.0 %all_to_all.20 = bf16[16,8,256]{2,1,0:T(8,128)(2,1)S(1)} all-to-all(bf16[16,8,256]{2,1,0:T(8,128)(2,1)S(1)} %bitcast.109), channel_id=1, replica_groups=mesh['dp_0a'=8,'dp_0b'=4,'dp_1'=2,'dp_2'=2,'tp'=8] {'dp_1','tp'}, dimensions={0} | all-to-all | bytes 131072 | tf_op jit(solution)/shard_map/all_to_all | solution.py:41
  14.9 51.9 %all_gather.3 = bf16[8,2,8,8,256]{4,3,2,1,0:T(8,128)(2,1)S(1)} all-gather(bf16[1,2,8,8,256]{4,3,2,1,0:T(8,128)(2,1)S(1)} %bitcast.108), channel_id=1, replica_groups=mesh['dp_0a'=8,'dp_0b'=4,'dp_1'=2,'dp_2'=2,'tp'=8] {'dp_0a'}, dimensions={0}, use_global_device_ids=true | all-gather | bytes 589824 | tf_op jit(solution)/shard_map/all_gather | solution.py:42
  66.8 1.6 %broadcast_in_dim.34 = bf16[4,8,2,8,8,256]{5,4,3,2,1,0:T(8,128)(2,1)} broadcast(bf16[8,2,8,8,256]{4,3,2,1,0:T(8,128)(2,1)S(1)} %all_gather.3), dimensions={1,2,3,4,5} | broadcast | bytes 2621440 | tf_op jit(solution)/shard_map/broadcast_in_dim | solution.py:32
  68.4 0.0 copy-start.2
  68.4 0.0 copy-start.5
  68.4 4.6 %all-to-all-start.1 = ((bf16[4,8,2,8,8,256]{5,4,3,2,1,0:T(8,128)(2,1)}), bf16[4,8,2,8,8,256]{5,4,3,2,1,0:T(8,128)(2,1)}, u32[]{:S(2)}, u32[]{:S(2)}) async-start(bf16[4,8,2,8,8,256]{5,4,3,2,1,0:T(8,128)(2,1)} %broadcast_in_dim.34), calls=%async_computation.1 | async-start | bytes 4194304 | tf_op jit(solution)/shard_map/all_to_all | solution.py:33
  72.9 0.0 copy-done.2
  72.9 0.1 copy.39
  73.0 0.0 copy-start.3
  73.0 0.0 copy-done.5
  73.1 0.1 iota_compare_fusion
  73.1 0.6 copy-done.3
  73.8 2.9 %fusion.26 = (f32[4,48,8]{2,0,1:T(4,128)S(1)}, f32[4,48,1,8,96]{4,3,0,1,2:T(8,128)}) fusion(bf16[48,1,2,96,128]{4,3,2,1,0:T(8,128)(2,1)} %param.9, pred[48,96]{1,0:T(8,128)(4,1)S(1)} %iota_compare_fusion, bf16[4,48,8,128]{3,2,1,0:T(8,128)(2,1)S(1)} %bitcast.106), kind=kOutput, calls=%fused_computation.41 | convolution fusion | flops 38189568 | bytes 2173440 | tf_op jit(solution)/shard_map/srgpe,rgce->srgpc/dot_general | solution.py:63
  76.7 43.7 %all-to-all-done.1 = bf16[4,8,2,8,8,256]{5,4,3,2,1,0:T(8,128)(2,1)} async-done(((bf16[4,8,2,8,8,256]{5,4,3,2,1,0:T(8,128)(2,1)}), bf16[4,8,2,8,8,256]{5,4,3,2,1,0:T(8,128)(2,1)}, u32[]{:S(2)}, u32[]{:S(2)}) %all-to-all-start.1) | async-done | bytes 2097184 | tf_op jit(solution)/shard_map/all_to_all | solution.py:33
  120.4 1.7 %copy.23 = bf16[4,8,2,8,8,256]{5,4,3,2,0,1:T(8,128)(2,1)S(1)} copy(bf16[4,8,2,8,8,256]{5,4,3,2,1,0:T(8,128)(2,1)} %all-to-all-done.1) | data formatting | bytes 4194304 | tf_op jit(solution)/shard_map/all_to_all | solution.py:33
  122.1 0.5 broadcast_in_dim.35
  122.6 8.5 %all_to_all.21 = bf16[2,4,8,2,8,8,256]{6,5,4,3,1,2,0:T(8,128)(2,1)S(1)} all-to-all(bf16[2,4,8,2,8,8,256]{6,5,4,3,1,2,0:T(8,128)(2,1)S(1)} %broadcast_in_dim.35), channel_id=1, replica_groups=mesh['dp_0a'=8,'dp_0b'=4,'dp_1'=2,'dp_2'=2,'tp'=8] {'dp_2'}, dimensions={0} | all-to-all | bytes 8388608 | tf_op jit(solution)/shard_map/all_to_all | solution.py:33
  131.2 0.6 copy.24
  131.7 0.0 copy-done
  131.8 1.1 convolution_convert_fusion
  132.9 0.0 copy-start.1
  132.9 0.1 fusion.25
  133.0 2.9 %fusion.27 = (f32[4,48,8]{2,0,1:T(4,128)S(1)}, f32[4,48,1,8,4]{3,4,0,1,2:T(4,128)S(1)}) fusion(bf16[4,48,1,1,128]{4,3,1,0,2:T(2,128)(2,1)S(1)} %get-tuple-element.6, pred[4,4]{1,0:T(4,128)(4,1)S(1)} %iota_compare_fusion.1, bf16[4,48,8,128]{3,2,1,0:T(8,128)(2,1)} %bitcast.107), kind=kOutput, calls=%fused_computation.42 | convolution fusion | flops 1589760 | bytes 473104 | tf_op jit(solution)/shard_map/srgpe,trge->srgpt/dot_general | solution.py:70
  136.0 0.4 fusion.21
  136.4 0.0 copy-start.6
  136.4 0.0 copy-done.1
  136.4 0.6 fusion.15
  137.0 0.4 fusion.22
  137.5 0.6 copy-done.6
  138.1 0.0 copy-start.4
  138.1 0.6 fusion.5
  138.7 0.8 reshape_reshape.3
  139.5 3.5 %all-to-all-start.3 = ((bf16[4,8,6,1024]{3,0,2,1:T(4,128)(2,1)}), bf16[4,8,6,1024]{3,0,2,1:T(4,128)(2,1)S(1)}, u32[]{:S(2)}, u32[]{:S(2)}) async-start(bf16[4,8,6,1024]{3,0,2,1:T(4,128)(2,1)} %reshape_reshape.3), calls=%async_computation.3 | async-start | bytes 786432 | tf_op jit(solution)/shard_map/all_to_all | solution.py:93
  143.0 0.0 copy-done.4
  143.0 0.6 reshape.150
  143.6 7.6 %all-to-all-done.3 = bf16[4,8,6,1024]{3,0,2,1:T(4,128)(2,1)S(1)} async-done(((bf16[4,8,6,1024]{3,0,2,1:T(4,128)(2,1)}), bf16[4,8,6,1024]{3,0,2,1:T(4,128)(2,1)S(1)}, u32[]{:S(2)}, u32[]{:S(2)}) %all-to-all-start.3) | async-done | bytes 393248 | tf_op jit(solution)/shard_map/all_to_all | solution.py:93
  151.1 0.3 fusion.12
  151.5 1.0 fusion.16
  152.5 0.9 copy.38
  (5 shorter events, 0.1 us)
Async XLA Ops:
  0.0 131.7 %copy-start = (bf16[4,48,8192]{2,1,0:T(8,128)(2,1)S(1)}, bf16[4,48,8192]{2,1,0:T(8,128)(2,1)}, u32[]{:S(2)}) copy-start(bf16[4,48,8192]{2,1,0:T(8,128)(2,1)} %param.6) | copy-start | bytes 9437188
  68.4 4.6 %copy-start.2 = (bf16[4,48,1024]{2,1,0:T(8,128)(2,1)S(1)}, bf16[4,48,1024]{2,1,0:T(8,128)(2,1)}, u32[]{:S(2)}) copy-start(bf16[4,48,1024]{2,1,0:T(8,128)(2,1)} %param.8) | copy-start | bytes 1179652
  68.4 4.7 %copy-start.5 = (s32[48]{0:T(128)S(1)}, s32[48]{0:T(128)}, u32[]{:S(2)}) copy-start(s32[48]{0:T(128)} %param.10) | copy-start | bytes 580
  68.4 52.0 %all-to-all-start.1 = ((bf16[4,8,2,8,8,256]{5,4,3,2,1,0:T(8,128)(2,1)}), bf16[4,8,2,8,8,256]{5,4,3,2,1,0:T(8,128)(2,1)}, u32[]{:S(2)}, u32[]{:S(2)}) async-start(bf16[4,8,2,8,8,256]{5,4,3,2,1,0:T(8,128)(2,1)} %broadcast_in_dim.34), calls=%async_computation.1 | async-start | bytes 4194304 | tf_op jit(solution)/shard_map/all_to_all | solution.py:33
  73.0 0.7 copy-start.3
  132.9 3.5 %copy-start.1 = (f32[4,48,1,8,96]{4,3,0,1,2:T(8,128)S(1)}, f32[4,48,1,8,96]{4,3,0,1,2:T(8,128)}, u32[]{:S(2)}) copy-start(f32[4,48,1,8,96]{4,3,0,1,2:T(8,128)} %get-tuple-element.8) | copy-start | bytes 1769476
  136.4 1.7 %copy-start.6 = (bf16[48,1,2,96,128]{4,3,2,1,0:T(8,128)(2,1)S(1)}, bf16[48,1,2,96,128]{4,3,2,1,0:T(8,128)(2,1)}, u32[]{:S(2)}) copy-start(bf16[48,1,2,96,128]{4,3,2,1,0:T(8,128)(2,1)} %param.9) | copy-start | bytes 7077892
  138.1 4.9 %copy-start.4 = (bf16[8192]{0:T(1024)(128)(2,1)S(1)}, bf16[8192]{0:T(1024)(128)(2,1)}, u32[]{:S(2)}) copy-start(bf16[8192]{0:T(1024)(128)(2,1)} %param.11) | copy-start | bytes 49156
  139.5 11.6 %all-to-all-start.3 = ((bf16[4,8,6,1024]{3,0,2,1:T(4,128)(2,1)}), bf16[4,8,6,1024]{3,0,2,1:T(4,128)(2,1)S(1)}, u32[]{:S(2)}, u32[]{:S(2)}) async-start(bf16[4,8,6,1024]{3,0,2,1:T(4,128)(2,1)} %reshape_reshape.3), calls=%async_computation.3 | async-start | bytes 786432 | tf_op jit(solution)/shard_map/all_to_all | solution.py:93

commit v6 on v5

--- a/solution.py
+++ b/solution.py
@@ -40,8 +40,9 @@
     spread = jnp.broadcast_to(mine[None], (2,) + mine.shape).reshape(2 * groups, rows, cols)
     t = lax.all_to_all(spread, ("dp_1", "tp"), 0, 0, tiled=True).reshape(2, groups, rows, cols)
     t = lax.all_gather(t, "dp_0a")
-    t = pp_gather(t, "dp_0b", 4)
-    t = pp_gather(t, "dp_2", 2)
+    shape = t.shape
+    t = pp_gather(t.reshape(-1, cols), "dp_0b", 4)
+    t = pp_gather(t.reshape(-1, cols), "dp_2", 2).reshape((2, 4) + shape)
     return t.transpose(2, 1, 3, 0, 4, 5, 6).reshape(-1, cols)
 
 def per_device(hidden, kv_weight, queries, kv_cache, lengths, out_gain):

time: 154 us -> 153 us (level)
    all_to_all x2 -> x0, local copies, waits for them, and re-layouts: 2.3 us -> none  [pp_gather(): return lax.all_to_all(spread, axis, 0, 0, tiled=True)]
where the time goes in v6:
time: 153 us
  blocking collectives  74.4 us (49%)
  waiting for transfers between devices  51.2 us (33%)
  local copies, waits for them, and re-layouts  8.64 us (6%)
  starting transfers between devices  8.02 us (5%)
  matrix products  7.97 us (5%)
  other arithmetic  2.45 us (2%)
    all_gather x1, blocking collectives, gather_w(): t = lax.all_gather(t, 'dp_0a')  51.9 us
    all_to_all x1, waiting for transfers between devices, pp_gather(): return lax.all_to_all(spread, axis, 0, 0, tiled=True)  43.7 us
    all_to_all x1, blocking collectives, gather_w(): lax.all_to_all(spread, ('dp_1', 'tp'), 0, 0, tiled=True)  14 us
    all_to_all x1, blocking collectives, pp_gather(): return lax.all_to_all(spread, axis, 0, 0, tiled=True)  8.52 us
    all_to_all x1, waiting for transfers between devices, per_device(): lax.all_to_all(blocks, 'tp', split_axis=1, concat_axis=1, tiled=True)  7.55 us
    all_to_all x1, starting transfers between devices, pp_gather(): return lax.all_to_all(spread, axis, 0, 0, tiled=True)  4.57 us
    all_to_all x1, starting transfers between devices, per_device(): lax.all_to_all(blocks, 'tp', split_axis=1, concat_axis=1, tiled=True)  3.45 us
    broadcast_in_dim x2, local copies, waits for them, and re-layouts, pp_gather(): spread = jnp.broadcast_to(x[None], (n,) + x.shape)  3.29 us
  transfers between devices with their start and end apart: 2, of which 2 were waited for; matrix products, arithmetic and copies ran while one was open for 2% of the time, Pallas kernels for 0%

profile of v6, /device:TPU:1, one launch (start us, length us, event | category | flops | bytes accessed | tf_op | source)
XLA Modules:
  0.0 152.9 jit_solution(10579331400361674882)
XLA Ops:
  0.0 0.0 copy-start
  0.0 0.9 broadcast_in_dim.58
  0.9 14.0 %all_to_all.20 = bf16[16,8,256]{2,1,0:T(8,128)(2,1)S(1)} all-to-all(bf16[16,8,256]{2,1,0:T(8,128)(2,1)S(1)} %bitcast.114), channel_id=1, replica_groups=mesh['dp_0a'=8,'dp_0b'=4,'dp_1'=2,'dp_2'=2,'tp'=8] {'dp_1','tp'}, dimensions={0} | all-to-all | bytes 131072 | tf_op jit(solution)/shard_map/all_to_all | solution.py:41
  14.9 51.9 %all_gather.3 = bf16[8,2,8,8,256]{4,3,2,1,0:T(8,128)(2,1)S(1)} all-gather(bf16[1,2,8,8,256]{4,3,2,1,0:T(8,128)(2,1)S(1)} %bitcast.113), channel_id=1, replica_groups=mesh['dp_0a'=8,'dp_0b'=4,'dp_1'=2,'dp_2'=2,'tp'=8] {'dp_0a'}, dimensions={0}, use_global_device_ids=true | all-gather | bytes 589824 | tf_op jit(solution)/shard_map/all_gather | solution.py:42
  66.8 1.4 broadcast_in_dim.60
  68.2 0.0 copy-start.2
  68.2 0.0 copy-start.5
  68.2 4.6 %all-to-all-start.1 = ((bf16[4,1024,256]{2,1,0:T(8,128)(2,1)}), bf16[4,1024,256]{2,1,0:T(8,128)(2,1)}, u32[]{:S(2)}, u32[]{:S(2)}) async-start(bf16[4,1024,256]{2,1,0:T(8,128)(2,1)} %broadcast_in_dim.60), calls=%async_computation.1 | async-start | bytes 4194304 | tf_op jit(solution)/shard_map/all_to_all | solution.py:33
  72.8 0.0 copy-done.2
  72.8 0.1 copy.46
  72.9 0.0 copy-start.3
  72.9 0.0 copy-done.5
  72.9 0.1 iota_compare_fusion
  73.0 0.6 copy-done.3
  73.6 2.9 %fusion.26 = (f32[4,48,8]{2,0,1:T(4,128)S(1)}, f32[4,48,1,8,96]{4,3,0,1,2:T(8,128)}) fusion(bf16[48,1,2,96,128]{4,3,2,1,0:T(8,128)(2,1)} %param.9, pred[48,96]{1,0:T(8,128)(4,1)S(1)} %iota_compare_fusion, bf16[4,48,8,128]{3,2,1,0:T(8,128)(2,1)S(1)} %bitcast.111), kind=kOutput, calls=%fused_computation.41 | convolution fusion | flops 38189568 | bytes 2173440 | tf_op jit(solution)/shard_map/srgpe,rgce->srgpc/dot_general | solution.py:64
  76.6 43.7 %all-to-all-done.1 = bf16[4,1024,256]{2,1,0:T(8,128)(2,1)} async-done(((bf16[4,1024,256]{2,1,0:T(8,128)(2,1)}), bf16[4,1024,256]{2,1,0:T(8,128)(2,1)}, u32[]{:S(2)}, u32[]{:S(2)}) %all-to-all-start.1) | async-done | bytes 2097184 | tf_op jit(solution)/shard_map/all_to_all | solution.py:33
  120.2 1.9 %broadcast_in_dim.62 = bf16[2,4096,256]{2,1,0:T(8,128)(2,1)S(1)} broadcast(bf16[4096,256]{1,0:T(8,128)(2,1)} %bitcast.11), dimensions={1,2} | broadcast | bytes 6291456 | tf_op jit(solution)/shard_map/broadcast_in_dim | solution.py:32
  122.1 8.5 %all_to_all.21 = bf16[2,4096,256]{2,1,0:T(8,128)(2,1)S(1)} all-to-all(bf16[2,4096,256]{2,1,0:T(8,128)(2,1)S(1)} %broadcast_in_dim.62), channel_id=1, replica_groups=mesh['dp_0a'=8,'dp_0b'=4,'dp_1'=2,'dp_2'=2,'tp'=8] {'dp_2'}, dimensions={0} | all-to-all | bytes 8388608 | tf_op jit(solution)/shard_map/all_to_all | solution.py:33
  130.6 0.6 copy.31
  131.2 0.0 copy-done
  131.2 1.1 convolution_convert_fusion
  132.3 0.0 copy-start.1
  132.4 0.1 fusion.25
  132.5 2.9 %fusion.27 = (f32[4,48,8]{2,0,1:T(4,128)S(1)}, f32[4,48,1,8,4]{3,4,0,1,2:T(4,128)S(1)}) fusion(bf16[4,48,1,1,128]{4,3,1,0,2:T(2,128)(2,1)S(1)} %get-tuple-element.6, pred[4,4]{1,0:T(4,128)(4,1)S(1)} %iota_compare_fusion.1, bf16[4,48,8,128]{3,2,1,0:T(8,128)(2,1)} %bitcast.112), kind=kOutput, calls=%fused_computation.42 | convolution fusion | flops 1589760 | bytes 473104 | tf_op jit(solution)/shard_map/srgpe,trge->srgpt/dot_general | solution.py:71
  135.5 0.4 fusion.21
  135.9 0.0 copy-start.6
  135.9 0.0 copy-done.1
  135.9 0.6 fusion.15
  136.5 0.4 fusion.22
  136.9 0.6 copy-done.6
  137.5 0.0 copy-start.4
  137.5 0.6 fusion.5
  138.1 0.8 reshape_reshape.3
  139.0 3.5 %all-to-all-start.3 = ((bf16[4,8,6,1024]{3,0,2,1:T(4,128)(2,1)}), bf16[4,8,6,1024]{3,0,2,1:T(4,128)(2,1)S(1)}, u32[]{:S(2)}, u32[]{:S(2)}) async-start(bf16[4,8,6,1024]{3,0,2,1:T(4,128)(2,1)} %reshape_reshape.3), calls=%async_computation.3 | async-start | bytes 786432 | tf_op jit(solution)/shard_map/all_to_all | solution.py:94
  142.4 0.0 copy-done.4
  142.4 0.6 reshape.154
  143.1 7.6 %all-to-all-done.3 = bf16[4,8,6,1024]{3,0,2,1:T(4,128)(2,1)S(1)} async-done(((bf16[4,8,6,1024]{3,0,2,1:T(4,128)(2,1)}), bf16[4,8,6,1024]{3,0,2,1:T(4,128)(2,1)S(1)}, u32[]{:S(2)}, u32[]{:S(2)}) %all-to-all-start.3) | async-done | bytes 393248 | tf_op jit(solution)/shard_map/all_to_all | solution.py:94
  150.6 0.3 fusion.12
  150.9 1.0 fusion.16
  152.0 0.9 copy.45
  (5 shorter events, 0.1 us)
Async XLA Ops:
  0.0 131.2 %copy-start = (bf16[4,48,8192]{2,1,0:T(8,128)(2,1)S(1)}, bf16[4,48,8192]{2,1,0:T(8,128)(2,1)}, u32[]{:S(2)}) copy-start(bf16[4,48,8192]{2,1,0:T(8,128)(2,1)} %param.6) | copy-start | bytes 9437188
  68.2 4.6 %copy-start.2 = (bf16[4,48,1024]{2,1,0:T(8,128)(2,1)S(1)}, bf16[4,48,1024]{2,1,0:T(8,128)(2,1)}, u32[]{:S(2)}) copy-start(bf16[4,48,1024]{2,1,0:T(8,128)(2,1)} %param.8) | copy-start | bytes 1179652
  68.2 4.7 %copy-start.5 = (s32[48]{0:T(128)S(1)}, s32[48]{0:T(128)}, u32[]{:S(2)}) copy-start(s32[48]{0:T(128)} %param.10) | copy-start | bytes 580
  68.2 52.0 %all-to-all-start.1 = ((bf16[4,1024,256]{2,1,0:T(8,128)(2,1)}), bf16[4,1024,256]{2,1,0:T(8,128)(2,1)}, u32[]{:S(2)}, u32[]{:S(2)}) async-start(bf16[4,1024,256]{2,1,0:T(8,128)(2,1)} %broadcast_in_dim.60), calls=%async_computation.1 | async-start | bytes 4194304 | tf_op jit(solution)/shard_map/all_to_all | solution.py:33
  72.9 0.7 copy-start.3
  132.3 3.5 %copy-start.1 = (f32[4,48,1,8,96]{4,3,0,1,2:T(8,128)S(1)}, f32[4,48,1,8,96]{4,3,0,1,2:T(8,128)}, u32[]{:S(2)}) copy-start(f32[4,48,1,8,96]{4,3,0,1,2:T(8,128)} %get-tuple-element.8) | copy-start | bytes 1769476
  135.9 1.7 %copy-start.6 = (bf16[48,1,2,96,128]{4,3,2,1,0:T(8,128)(2,1)S(1)}, bf16[48,1,2,96,128]{4,3,2,1,0:T(8,128)(2,1)}, u32[]{:S(2)}) copy-start(bf16[48,1,2,96,128]{4,3,2,1,0:T(8,128)(2,1)} %param.9) | copy-start | bytes 7077892
  137.5 4.9 %copy-start.4 = (bf16[8192]{0:T(1024)(128)(2,1)S(1)}, bf16[8192]{0:T(1024)(128)(2,1)}, u32[]{:S(2)}) copy-start(bf16[8192]{0:T(1024)(128)(2,1)} %param.11) | copy-start | bytes 49156
  139.0 11.6 %all-to-all-start.3 = ((bf16[4,8,6,1024]{3,0,2,1:T(4,128)(2,1)}), bf16[4,8,6,1024]{3,0,2,1:T(4,128)(2,1)S(1)}, u32[]{:S(2)}, u32[]{:S(2)}) async-start(bf16[4,8,6,1024]{3,0,2,1:T(4,128)(2,1)} %reshape_reshape.3), calls=%async_computation.3 | async-start | bytes 786432 | tf_op jit(solution)/shard_map/all_to_all | solution.py:94
